TPU v7x, 32 devices: a whole 2x2x4 slice. The times are simulated.
32 devices in a mesh: gx: 8 (over z, x), gy: 4 (over y, core).
Axes of the slice: x: 2, y: 2, z: 4, core: 2. Of those that a mesh axis runs over, the one named last changes fastest.
Arguments:
- solution: float32 [4, 16, 5120], P(None, 'gx', 'gy'), may hold values from -0.12 to 0.12
- forcing: float32 [4, 16, 5120], P(None, 'gx', 'gy'), may hold values from -0.12 to 0.12
- viscosity: float32 [16, 5120], P('gx', 'gy'), may hold values from 0.3 to 1
- blocks: float32 [16, 16, 5120], P(None, 'gx', 'gy'), may hold values from -0.5 to 0.5, as said below
- layer_count: int32 [16, 64], P('gx', 'gy'), may hold values from 40 to 80
- bed_frozen: int32 [16, 64], P('gx', 'gy'), may hold values 0 or 1
- basin_map: int32 [16, 64], P('gx', 'gy'), may hold values from 0 to 15, as said below
Outputs:
- smoothed: float32 [4, 16, 5120], P(None, 'gx', 'gy')
- column_residual: float32 [4, 16, 64], P(None, 'gx', 'gy')
- basin_residual: float32 [4, 16], replicated
Inputs may be any that keep to these rules, and one draw needn't show every extreme that they name: `blocks`: the first three diagonal entries of every cell's block are positive. `basin_map`: every basin number names some column.
All inputs are finite; a program needn't handle non-finite values. No bound on the sum of `bed_frozen` on one device may be relied on, other than what follows from the above.
Results may differ from a plain program's by a relative error of at most 0.00045.
Values sent between devices are 32-bit elements; how exact they have to be, the bound alone decides.
No kernel may reach another device: no remote copies, remote signals or barrier semaphores. Data moves between devices by JAX's collectives and lax.ppermute only.
A program may use at most 64 MiB of HBM per device.

v0:
```python
import jax
import jax.numpy as jnp
from jax import lax
from jax.sharding import PartitionSpec as P

LAYERS = 80


coupling = 0.25


def with_halo(block, sides, width):
    for axis, dim in sides:
        count = lax.axis_size(axis)
        forward = [(i, i + 1) for i in range(count - 1)]
        backward = [(target, source) for source, target in forward]
        low = lax.ppermute(
            lax.slice_in_dim(block, block.shape[dim] - width, None, axis=dim), axis, forward
        )
        high = lax.ppermute(lax.slice_in_dim(block, 0, width, axis=dim), axis, backward)
        block = jnp.concatenate([low, block, high], axis=dim)
    return block


def carried_in(value, axis, join, neutral, backward):
    count, mine = (lax.axis_size(axis), lax.axis_index(axis))
    pieces = lax.all_gather(value, axis)
    if backward:
        pieces = pieces[::-1]
        mine = count - 1 - mine
    running = jnp.full_like(value, 0) + jnp.asarray(neutral, value.dtype)

    def lap(position, running):
        longer = join(running, pieces[position])
        return jnp.where(position < mine, longer, running)

    return lax.fori_loop(0, count - 1, lap, running)


def vertical_pair(grid_view, frozen):
    lower_cells = jnp.concatenate(
        [grid_view[..., :1] * (1.0 - frozen)[None, :, :, None], grid_view[..., :-1]], axis=-1
    )
    upper_cells = jnp.concatenate([grid_view[..., 1:], jnp.zeros_like(grid_view[..., :1])], axis=-1)
    return lower_cells + upper_cells


def neighbour_terms(velocity, viscosity, frozen):
    grid_view = velocity.reshape(3, velocity.shape[1], velocity.shape[2] // LAYERS, LAYERS)
    padded = with_halo(grid_view, (("gx", 1), ("gy", 2)), 1)
    along_line = 2.0 * grid_view - padded[:, :-2, 1:-1] - padded[:, 2:, 1:-1]
    across_line = padded[:, 1:-1, :-2] + padded[:, 1:-1, 2:] + vertical_pair(grid_view, frozen)
    return viscosity * along_line.reshape(
        velocity.shape
    ) - coupling * viscosity * across_line.reshape(velocity.shape)


def operate(masked, matrix, viscosity, frozen):
    in_cell = jnp.sum(matrix * masked[None], axis=1)
    moving = in_cell[:3] + neighbour_terms(masked[:3], viscosity, frozen)
    return jnp.concatenate([moving, in_cell[3:]], axis=0)


def pair_product(later, earlier):
    entries = jnp.stack(
        [
            later[0] * earlier[0] + later[1] * earlier[2],
            later[0] * earlier[1] + later[1] * earlier[3],
            later[2] * earlier[0] + later[3] * earlier[2],
            later[2] * earlier[1] + later[3] * earlier[3],
        ]
    )
    return entries / jnp.max(jnp.abs(entries), axis=0)


def affine_pair(later, earlier):
    return jnp.stack([later[0] * earlier[0], later[0] * earlier[1] + later[1]])


def chain_pivots(earlier, later):
    return pair_product(later, earlier)


def chain_affine(earlier, later):
    return affine_pair(later, earlier)


def local_pivots(line_lead, line_off, gain_prev):
    gains = []
    pivots = []
    for cell_idx in range(line_lead.shape[1]):
        pivot = line_lead[:, cell_idx] - line_off[:, cell_idx] * gain_prev
        gain_prev = line_off[:, cell_idx] / pivot
        gains.append(gain_prev)
        pivots.append(pivot)
    return (gains, pivots)


def forward_values(line_rhs, line_off, pivots, value_prev):
    values = []
    for cell_idx in range(line_rhs.shape[1]):
        value_prev = (line_rhs[:, cell_idx] + line_off[:, cell_idx] * value_prev) / pivots[cell_idx]
        values.append(value_prev)
    return values


def back_maps(gains, values, ones_line, zeros_line):
    unit_back = jnp.stack([ones_line, zeros_line])
    back_map = unit_back
    for cell_idx in reversed(range(len(values))):
        back_map = affine_pair(jnp.stack([gains[cell_idx], values[cell_idx]]), back_map)
    return (back_map, unit_back)


def back_values(gains, values, next_value):
    corrections = list(values)
    for cell_idx in reversed(range(len(values))):
        next_value = values[cell_idx] + gains[cell_idx] * next_value
        corrections[cell_idx] = next_value
    return jnp.stack(corrections, axis=1)


def local(solution, forcing, viscosity, blocks, layer_count, bed_frozen, basin_map):
    row_count = solution.shape[1]
    lane_count = solution.shape[2]
    y_cells = lane_count // LAYERS
    layer_idx = jnp.arange(LAYERS, dtype=jnp.int32)
    active = (
        (layer_idx[None, None, :] < layer_count[:, :, None])
        .astype(jnp.float32)
        .reshape(row_count, lane_count)
    )
    frozen = bed_frozen.astype(jnp.float32)
    matrix = blocks.reshape(4, 4, row_count, lane_count)
    masked = solution * active[None]
    residual = active[None] * (forcing - operate(masked, matrix, viscosity, frozen))
    diagonal = jnp.stack([matrix[0, 0], matrix[1, 1], matrix[2, 2]])
    line_lead = jnp.where(active[None] > 0.0, diagonal + 2.0 * viscosity[None], 1.0)
    line_off = jnp.broadcast_to((viscosity * active)[None], line_lead.shape)
    line_rhs = residual[:3]
    ones_line = jnp.ones_like(line_rhs[:, 0])
    zeros_line = jnp.zeros_like(line_rhs[:, 0])
    unit_pair = jnp.stack([ones_line, zeros_line, zeros_line, ones_line])
    composite = unit_pair
    for cell_idx in range(row_count):
        off_cell = line_off[:, cell_idx]
        cell_map = jnp.stack([zeros_line, off_cell, -off_cell, line_lead[:, cell_idx]])
        composite = pair_product(cell_map, composite)
    incoming = carried_in(composite, "gx", chain_pivots, unit_pair, False)
    gains, pivots = local_pivots(line_lead, line_off, incoming[1] / incoming[3])
    unit_shift = jnp.stack([ones_line, zeros_line])
    shift_map = unit_shift
    for cell_idx in range(row_count):
        cell_map = jnp.stack([gains[cell_idx], line_rhs[:, cell_idx] / pivots[cell_idx]])
        shift_map = affine_pair(cell_map, shift_map)
    value_prev = carried_in(shift_map, "gx", chain_affine, unit_shift, False)[1]
    values = forward_values(line_rhs, line_off, pivots, value_prev)
    back_map, unit_back = back_maps(gains, values, ones_line, zeros_line)
    next_value = carried_in(back_map, "gx", chain_affine, unit_back, True)[1]
    correction = back_values(gains, values, next_value)
    pressure_in = residual[3] - (
        matrix[3, 0] * correction[0] + matrix[3, 1] * correction[1] + matrix[3, 2] * correction[2]
    )
    pressure_step = active * pressure_in / viscosity
    full_step = jnp.concatenate([correction, pressure_step[None]], axis=0)
    smoothed = solution + full_step
    post = active[None] * (forcing - operate(smoothed * active[None], matrix, viscosity, frozen))
    column_residual = jnp.sum(post.reshape(4, row_count, y_cells, LAYERS), axis=-1)
    basin_count = lax.axis_size("gx") // 2 * lax.axis_size("gy")
    member_table = (
        basin_map.reshape(-1)[:, None] == jnp.arange(basin_count, dtype=jnp.int32)[None, :]
    ).astype(jnp.float32)
    partial_sums = jnp.dot(
        column_residual.reshape(4, -1),
        member_table,
        precision=lax.Precision.HIGHEST,
        preferred_element_type=jnp.float32,
    )
    basin_residual = lax.psum(partial_sums, ("gx", "gy"))
    return (smoothed, column_residual, basin_residual)


def solution(mesh):
    return jax.shard_map(
        local,
        mesh=mesh,
        in_specs=(
            P(None, "gx", "gy"),
            P(None, "gx", "gy"),
            P("gx", "gy"),
            P(None, "gx", "gy"),
            P("gx", "gy"),
            P("gx", "gy"),
            P("gx", "gy"),
        ),
        out_specs=(P(None, "gx", "gy"), P(None, "gx", "gy"), P()),
        check_vma=False,
    )
```

profile of v0, /device:TPU:0, one launch (start us, length us, event | category | flops | bytes accessed | tf_op | source)
XLA Modules:
  0.0 176.3 jit_solution(14619022692463178866)
XLA Ops:
  0.6 0.7 lt.82
  1.4 0.1 lt.83
  1.5 0.1 lt.80
  1.6 0.7 copy-done.8
  2.3 0.1 reshape.379
  2.5 4.9 %collective-permute-start = (f32[3,1,16,80]{3,2,1,0:T(8,128)S(1)}, f32[3,1,16,80]{3,2,1,0:T(8,128)S(1)}, u32[]{:S(2)}, u32[]{:S(2)}) collective-permute-start(f32[3,1,16,80]{3,2,1,0:T(8,128)S(1)} %get-tuple-element.329), channel_id=1, source_target_pairs={{0,4},{4,8},{8,12},{12,16},{16,20},{20,24},{24,28},{1,5},{5,9},{9,... | collective-permute-start | bytes 46088 | tf_op jit(solution)/shard_map/ppermute | solution.py:17
  7.4 1.4 collective-permute-start.1
  8.8 0.1 fusion.57
  8.9 0.1 slice_multiply_fusion.3
  9.0 0.7 copy-done.5
  9.8 0.1 multiply_reduce_fusion.1
  9.9 3.4 %collective-permute-done.1 = f32[3,1,16,80]{3,2,1,0:T(8,128)S(1)} collective-permute-done((f32[3,1,16,80]{3,2,1,0:T(8,128)S(1)}, f32[3,1,16,80]{3,2,1,0:T(8,128)S(1)}, u32[]{:S(2)}, u32[]{:S(2)}) %collective-permute-start.1) | collective-permute-done | bytes 15392 | tf_op jit(solution)/shard_map/ppermute | solution.py:20
  13.3 1.3 collective-permute-start.2
  14.6 1.3 collective-permute-start.3
  15.9 0.8 copy-done.9
  16.7 0.6 copy-done.1
  17.3 0.1 copy-done.12
  17.4 0.1 eq.15
  17.5 0.1 reshape.380
  17.6 1.8 %collective-permute-done.3 = f32[3,4,1,80]{3,2,1,0:T(1,128)S(1)} collective-permute-done((f32[3,4,1,80]{3,2,1,0:T(1,128)S(1)}, f32[3,4,1,80]{3,2,1,0:T(1,128)S(1)}, u32[]{:S(2)}, u32[]{:S(2)}) %collective-permute-start.3) | collective-permute-done | bytes 3872 | tf_op jit(solution)/shard_map/ppermute | solution.py:20
  19.4 0.1 fusion.20
  19.5 0.1 reshape.381
  19.7 0.1 abs_reduce_fusion.1
  19.8 0.1 broadcast_divide_fusion
  19.9 0.1 multiply_add_fusion.3
  20.0 0.1 fusion.14
  20.1 0.1 maximum_divide_fusion
  20.2 31.6 %all_gather.16 = f32[8,4,3,1280]{3,1,2,0:T(4,128)S(1)} all-gather(f32[1,4,3,1280]{3,1,2,0:T(4,128)S(1)} %maximum_divide_fusion), channel_id=1, replica_groups=mesh['gx'=8,'gy'=4] {'gx'}, dimensions={0}, use_global_device_ids=true | all-gather | bytes 552960 | tf_op jit(solution)/shard_map/all_gather | solution.py:27
  51.8 1.5 while.39
  52.1 0.1 constant_dynamic-slice_fusion.5
  52.3 0.1 constant_dynamic-slice_fusion.5
  52.5 0.1 constant_dynamic-slice_fusion.5
  52.7 0.1 constant_dynamic-slice_fusion.5
  52.9 0.1 constant_dynamic-slice_fusion.5
  53.5 0.7 copy-done.6
  54.2 0.1 fusion.31
  54.4 31.1 %all-gather = f32[16,3,1280]{2,1,0:T(4,128)S(1)} all-gather(f32[2,3,1280]{2,1,0:T(4,128)S(1)} %copy.23), channel_id=2, replica_groups=mesh['gx'=8,'gy'=4] {'gx'}, dimensions={0}, use_global_device_ids=true | all-gather | bytes 276480 | tf_op jit(solution)/shard_map/all_gather | solution.py:27
  85.5 0.5 while.40
  86.0 0.1 multiply_add_fusion.1
  86.2 30.9 %all-gather.1 = f32[16,3,1280]{2,1,0:T(4,128)S(1)} all-gather(f32[2,3,1280]{2,1,0:T(4,128)S(1)} %copy.25), channel_id=3, replica_groups=mesh['gx'=8,'gy'=4] {'gx'}, dimensions={0}, use_global_device_ids=true | all-gather | bytes 276480 | tf_op jit(solution)/shard_map/all_gather | solution.py:27
  117.1 0.7 copy-done.2
  117.8 0.5 while.41
  118.3 0.1 multiply_add_fusion
  118.5 0.7 broadcast_multiply_fusion
  119.2 0.1 reshape.382
  119.3 0.1 fusion.55
  119.4 2.1 %collective-permute-start.4 = (f32[3,1,16,80]{3,2,1,0:T(8,128)S(1)}, f32[3,1,16,80]{3,2,1,0:T(8,128)S(1)}, u32[]{:S(2)}, u32[]{:S(2)}) collective-permute-start(f32[3,1,16,80]{3,2,1,0:T(8,128)S(1)} %get-tuple-element.323), channel_id=1, source_target_pairs={{0,4},{4,8},{8,12},{12,16},{16,20},{20,24},{24,28},{1,5},{5,9},{9,... | collective-permute-start | bytes 46088 | tf_op jit(solution)/shard_map/ppermute | solution.py:17
  121.5 0.1 slice_multiply_fusion.2
  121.5 1.3 collective-permute-start.5
  122.8 0.1 collective-permute-done.4
  123.0 4.3 %collective-permute-done.5 = f32[3,1,16,80]{3,2,1,0:T(8,128)S(1)} collective-permute-done((f32[3,1,16,80]{3,2,1,0:T(8,128)S(1)}, f32[3,1,16,80]{3,2,1,0:T(8,128)S(1)}, u32[]{:S(2)}, u32[]{:S(2)}) %collective-permute-start.5) | collective-permute-done | bytes 15392 | tf_op jit(solution)/shard_map/ppermute | solution.py:20
  127.3 1.3 collective-permute-start.6
  128.6 1.3 collective-permute-start.7
  129.9 0.1 multiply_reduce_fusion
  130.0 0.1 reshape.383
  130.1 4.4 %collective-permute-done.7 = f32[3,4,1,80]{3,2,1,0:T(1,128)S(1)} collective-permute-done((f32[3,4,1,80]{3,2,1,0:T(1,128)S(1)}, f32[3,4,1,80]{3,2,1,0:T(1,128)S(1)}, u32[]{:S(2)}, u32[]{:S(2)}) %collective-permute-start.7) | collective-permute-done | bytes 3872 | tf_op jit(solution)/shard_map/ppermute | solution.py:20
  134.5 0.1 fusion.16
  134.6 0.1 reshape.384
  134.8 0.1 reshape.385
  134.9 0.1 reduce_sum.29
  135.0 0.1 reshape.386
  135.1 0.2 fusion.26
  135.3 0.3 copy-done.10
  135.6 40.7 %psum.7 = f32[4,16]{1,0:T(4,128)} all-reduce(f32[4,16]{1,0:T(4,128)S(1)} %fusion.26), channel_id=1, replica_groups=mesh['gx'=8,'gy'=4] {'gx','gy'}, use_global_device_ids=true, to_apply=%region_12.13 | all-reduce | flops 64 | bytes 512 | tf_op jit(solution)/shard_map/psum | solution.py:179
  (118 shorter events, 2.5 us)
Async XLA Ops:
  1.6 0.8 copy-start.8
  2.5 7.4 %collective-permute-start = (f32[3,1,16,80]{3,2,1,0:T(8,128)S(1)}, f32[3,1,16,80]{3,2,1,0:T(8,128)S(1)}, u32[]{:S(2)}, u32[]{:S(2)}) collective-permute-start(f32[3,1,16,80]{3,2,1,0:T(8,128)S(1)} %get-tuple-element.329), channel_id=1, source_target_pairs={{0,4},{4,8},{8,12},{12,16},{16,20},{20,24},{24,28},{1,5},{5,9},{9,... | collective-permute-start | bytes 46088 | tf_op jit(solution)/shard_map/ppermute | solution.py:17
  7.3 1.5 copy-start.11
  7.4 2.3 %copy-start.4 = (f32[16,2,1280]{2,1,0:T(2,128)S(1)}, f32[16,2,1280]{2,1,0:T(2,128)}, u32[]{:S(2)}) copy-start(f32[16,2,1280]{2,1,0:T(2,128)} %param.16) | copy-start | bytes 491524
  7.4 5.9 %collective-permute-start.1 = (f32[3,1,16,80]{3,2,1,0:T(8,128)S(1)}, f32[3,1,16,80]{3,2,1,0:T(8,128)S(1)}, u32[]{:S(2)}, u32[]{:S(2)}) collective-permute-start(f32[3,1,16,80]{3,2,1,0:T(8,128)S(1)} %get-tuple-element.328), channel_id=1, source_target_pairs={{4,0},{8,4},{12,8},{16,12},{20,16},{24,20},{28,24},{5,1},{9,5},{13... | collective-permute-start | bytes 46088 | tf_op jit(solution)/shard_map/ppermute | solution.py:20
  9.0 0.7 copy-start.5
  9.8 9.8 %copy-start.7 = (f32[4,2,1280]{2,1,0:T(2,128)}, f32[4,2,1280]{2,1,0:T(2,128)S(1)}, u32[]{:S(2)}) copy-start(f32[4,2,1280]{2,1,0:T(2,128)S(1)} %multiply_reduce_fusion.1) | copy-start | bytes 122884
  13.3 4.3 %collective-permute-start.2 = (f32[3,4,1,80]{3,2,1,0:T(1,128)S(1)}, f32[3,4,1,80]{3,2,1,0:T(1,128)S(1)}, u32[]{:S(2)}, u32[]{:S(2)}) collective-permute-start(f32[3,4,1,80]{3,2,1,0:T(1,128)S(1)} %get-tuple-element.312), channel_id=1, source_target_pairs={{0,1},{1,2},{2,3},{4,5},{5,6},{6,7},{8,9},{9,10},{10,11},{12,13},{... | collective-permute-start | bytes 11528 | tf_op jit(solution)/shard_map/ppermute | solution.py:17
  14.6 4.8 %collective-permute-start.3 = (f32[3,4,1,80]{3,2,1,0:T(1,128)S(1)}, f32[3,4,1,80]{3,2,1,0:T(1,128)S(1)}, u32[]{:S(2)}, u32[]{:S(2)}) collective-permute-start(f32[3,4,1,80]{3,2,1,0:T(1,128)S(1)} %get-tuple-element.313), channel_id=1, source_target_pairs={{1,0},{2,1},{3,2},{5,4},{6,5},{7,6},{9,8},{10,9},{11,10},{13,12},{... | collective-permute-start | bytes 11528 | tf_op jit(solution)/shard_map/ppermute | solution.py:20
  15.9 0.8 copy-start.9
  16.7 0.6 copy-start.1
  16.7 0.7 copy-start.12
  20.2 31.6 %copy-start = (f32[4,3,1280]{2,1,0:T(4,128)S(1)}, f32[4,3,1280]{2,1,0:T(4,128)}, u32[]{:S(2)}) copy-start(f32[4,3,1280]{2,1,0:T(4,128)} %constant.98.clone.1) | copy-start | bytes 184324
  53.4 0.8 copy-start.6
  53.4 0.8 slice-start
  54.4 31.1 %copy-start.3 = (f32[2,3,1280]{2,1,0:T(4,128)S(1)}, f32[2,3,1280]{2,1,0:T(4,128)}, u32[]{:S(2)}) copy-start(f32[2,3,1280]{2,1,0:T(4,128)} %copy-done.1) | copy-start | bytes 92164
  117.0 0.8 copy-start.2
  119.4 3.6 %collective-permute-start.4 = (f32[3,1,16,80]{3,2,1,0:T(8,128)S(1)}, f32[3,1,16,80]{3,2,1,0:T(8,128)S(1)}, u32[]{:S(2)}, u32[]{:S(2)}) collective-permute-start(f32[3,1,16,80]{3,2,1,0:T(8,128)S(1)} %get-tuple-element.323), channel_id=1, source_target_pairs={{0,4},{4,8},{8,12},{12,16},{16,20},{20,24},{24,28},{1,5},{5,9},{9,... | collective-permute-start | bytes 46088 | tf_op jit(solution)/shard_map/ppermute | solution.py:17
  121.5 5.7 %collective-permute-start.5 = (f32[3,1,16,80]{3,2,1,0:T(8,128)S(1)}, f32[3,1,16,80]{3,2,1,0:T(8,128)S(1)}, u32[]{:S(2)}, u32[]{:S(2)}) collective-permute-start(f32[3,1,16,80]{3,2,1,0:T(8,128)S(1)} %get-tuple-element.322), channel_id=1, source_target_pairs={{4,0},{8,4},{12,8},{16,12},{20,16},{24,20},{28,24},{5,1},{9,5},{13... | collective-permute-start | bytes 46088 | tf_op jit(solution)/shard_map/ppermute | solution.py:20
  127.3 2.8 %collective-permute-start.6 = (f32[3,4,1,80]{3,2,1,0:T(1,128)S(1)}, f32[3,4,1,80]{3,2,1,0:T(1,128)S(1)}, u32[]{:S(2)}, u32[]{:S(2)}) collective-permute-start(f32[3,4,1,80]{3,2,1,0:T(1,128)S(1)} %get-tuple-element.310), channel_id=1, source_target_pairs={{0,1},{1,2},{2,3},{4,5},{5,6},{6,7},{8,9},{9,10},{10,11},{12,13},{... | collective-permute-start | bytes 11528 | tf_op jit(solution)/shard_map/ppermute | solution.py:17
  128.6 5.9 %collective-permute-start.7 = (f32[3,4,1,80]{3,2,1,0:T(1,128)S(1)}, f32[3,4,1,80]{3,2,1,0:T(1,128)S(1)}, u32[]{:S(2)}, u32[]{:S(2)}) collective-permute-start(f32[3,4,1,80]{3,2,1,0:T(1,128)S(1)} %get-tuple-element.311), channel_id=1, source_target_pairs={{1,0},{2,1},{3,2},{5,4},{6,5},{7,6},{9,8},{10,9},{11,10},{13,12},{... | collective-permute-start | bytes 11528 | tf_op jit(solution)/shard_map/ppermute | solution.py:20
  135.0 0.6 copy-start.10
where the time goes:
time: 177 us; the launch traced here: 176 us
  blocking collectives  134 us (76%)
  starting transfers between devices  14.8 us (8%)
  waiting for transfers between devices  13.9 us (8%)
  local copies, waits for them, and re-layouts  7.38 us (4%)
  other arithmetic  4.04 us (2%)
    all_gather x3, blocking collectives, carried_in(): pieces = lax.all_gather(value, axis)  93.5 us
    psum x1, blocking collectives, local(): basin_residual = lax.psum(partial_sums, ('gx', 'gy'))  40.7 us
    ppermute x4, waiting for transfers between devices, with_halo(): lax.ppermute(lax.slice_in_dim(block, 0, width, axis=dim), axis, backward)  13.8 us
    ppermute x4, starting transfers between devices, with_halo(): lax.ppermute(lax.slice_in_dim(block, block.shape[dim] - width, None, axis...  9.52 us
    ppermute x4, starting transfers between devices, with_halo(): lax.ppermute(lax.slice_in_dim(block, 0, width, axis=dim), axis, backward)  5.29 us
    unnamed x30, local copies, waits for them, and re-layouts  4.69 us
  transfers between devices with their start and end apart: 8, of which 5 were waited for; matrix products, arithmetic and copies ran while one was open for 0% of the time, Pallas kernels for 0%

commit v1 on v0

v1 whole, which is shorter than its diff:
```python
import jax
import jax.numpy as jnp
from jax import lax
from jax.sharding import PartitionSpec as P

LAYERS = 80


coupling = 0.25


def neighbour_shift(block, axis, dim, width):
    count = lax.axis_size(axis)
    forward = [(i, i + 1) for i in range(count - 1)]
    backward = [(target, source) for source, target in forward]
    low = lax.ppermute(lax.slice_in_dim(block, block.shape[dim] - width, None, axis=dim), axis, forward)
    high = lax.ppermute(lax.slice_in_dim(block, 0, width, axis=dim), axis, backward)
    return low, high


def vertical_pair(grid_view, frozen):
    lower_cells = jnp.concatenate(
        [grid_view[..., :1] * (1.0 - frozen)[None, :, :, None], grid_view[..., :-1]], axis=-1
    )
    upper_cells = jnp.concatenate([grid_view[..., 1:], jnp.zeros_like(grid_view[..., :1])], axis=-1)
    return lower_cells + upper_cells


def neighbour_terms(grid_view, x_low, x_high, y_low, y_high, viscosity, frozen):
    shape = grid_view.shape
    x_pad = jnp.concatenate([x_low, grid_view, x_high], axis=1)
    y_pad = jnp.concatenate([y_low, grid_view, y_high], axis=2)
    along_line = 2.0 * grid_view - x_pad[:, :-2] - x_pad[:, 2:]
    across_line = y_pad[:, :, :-2] + y_pad[:, :, 2:] + vertical_pair(grid_view, frozen)
    flat = (3, shape[1], shape[2] * shape[3])
    return viscosity * along_line.reshape(flat) - coupling * viscosity * across_line.reshape(flat)


def in_cell_terms(masked, matrix):
    return jnp.sum(matrix * masked[None], axis=1)


def gather_rows(block, axis):
    count, mine = (lax.axis_size(axis), lax.axis_index(axis))
    if count > 8:
        return lax.all_gather(block, axis, axis=1, tiled=True)
    pieces = [block]
    for step in range(1, count):
        pairs = [((i + step) % count, i) for i in range(count)]
        pieces.append(lax.ppermute(block, axis, pairs))
    stacked = jnp.stack(pieces + pieces, axis=0)
    ordered = lax.dynamic_slice_in_dim(stacked, count - mine, count, axis=0)
    ordered = jnp.moveaxis(ordered, 0, 1)
    return ordered.reshape(block.shape[0], count * block.shape[1], *block.shape[2:])


def line_solve(line_lead, line_off, line_rhs):
    rows = line_lead.shape[1]
    gain_prev = jnp.zeros_like(line_rhs[:, 0])
    value_prev = jnp.zeros_like(line_rhs[:, 0])
    gains, values = [], []
    for cell_idx in range(rows):
        off_cell = line_off[:, cell_idx]
        pivot = line_lead[:, cell_idx] - off_cell * gain_prev
        gain_prev = off_cell / pivot
        value_prev = (line_rhs[:, cell_idx] + off_cell * value_prev) / pivot
        gains.append(gain_prev)
        values.append(value_prev)
    next_value = jnp.zeros_like(line_rhs[:, 0])
    corrections = list(values)
    for cell_idx in reversed(range(rows)):
        next_value = values[cell_idx] + gains[cell_idx] * next_value
        corrections[cell_idx] = next_value
    return jnp.stack(corrections, axis=1)


def line_solve_scan(line_lead, line_off, line_rhs):
    def sweep_down(carried, cell_cols):
        gain_prev, value_prev = carried
        lead_cell, off_cell, rhs_cell = cell_cols
        pivot = lead_cell - off_cell * gain_prev
        gain = off_cell / pivot
        value = (rhs_cell + off_cell * value_prev) / pivot
        return (gain, value), (gain, value)

    zeros_line = jnp.zeros_like(line_rhs[:, 0])
    scanned = (jnp.moveaxis(line_lead, 1, 0), jnp.moveaxis(line_off, 1, 0), jnp.moveaxis(line_rhs, 1, 0))
    _, (gains, values) = lax.scan(sweep_down, (zeros_line, zeros_line), scanned)

    def sweep_up(next_value, cell_cols):
        gain, value = cell_cols
        solved = value + gain * next_value
        return solved, solved

    _, corrections = lax.scan(sweep_up, zeros_line, (gains, values), reverse=True)
    return jnp.moveaxis(corrections, 0, 1)


def tree_sum(value, axis):
    count = lax.axis_size(axis)
    if count & (count - 1):
        return lax.psum(value, axis)
    step = 1
    while step < count:
        value = value + lax.ppermute(value, axis, [(i, i ^ step) for i in range(count)])
        step *= 2
    return value


def local(solution, forcing, viscosity, blocks, layer_count, bed_frozen, basin_map):
    row_count = solution.shape[1]
    lane_count = solution.shape[2]
    y_cells = lane_count // LAYERS
    layer_idx = jnp.arange(LAYERS, dtype=jnp.int32)
    active = (
        (layer_idx[None, None, :] < layer_count[:, :, None])
        .astype(jnp.float32)
        .reshape(row_count, lane_count)
    )
    frozen = bed_frozen.astype(jnp.float32)
    matrix = blocks.reshape(4, 4, row_count, lane_count)
    grid = (3, row_count, y_cells, LAYERS)

    masked = solution * active[None]
    masked_grid = masked[:3].reshape(grid)
    x_low, x_high = neighbour_shift(masked_grid, "gx", 1, 1)
    y_low, y_high = neighbour_shift(masked_grid, "gy", 2, 1)
    in_cell = in_cell_terms(masked, matrix)
    moving = in_cell[:3] + neighbour_terms(masked_grid, x_low, x_high, y_low, y_high, viscosity, frozen)
    residual = active[None] * (forcing - jnp.concatenate([moving, in_cell[3:]], axis=0))

    diagonal = jnp.stack([matrix[0, 0], matrix[1, 1], matrix[2, 2]])
    line_lead = jnp.where(active[None] > 0.0, diagonal + 2.0 * viscosity[None], 1.0)
    line_off = (viscosity * active)[None]
    packed = jnp.concatenate([line_lead, line_off, residual[:3]], axis=0)
    whole = gather_rows(packed, "gx")
    all_rows = whole.shape[1]
    solver = line_solve if all_rows <= 32 else line_solve_scan
    whole_corr = solver(whole[0:3], jnp.broadcast_to(whole[3:4], (3,) + whole.shape[1:]), whole[4:7])

    first = lax.axis_index("gx") * row_count
    padded_corr = jnp.pad(whole_corr, ((0, 0), (1, 1), (0, 0)))
    near_corr = lax.dynamic_slice_in_dim(padded_corr, first, row_count + 2, axis=1)
    correction = near_corr[:, 1:-1]

    pressure_in = residual[3] - (
        matrix[3, 0] * correction[0] + matrix[3, 1] * correction[1] + matrix[3, 2] * correction[2]
    )
    pressure_step = active * pressure_in / viscosity
    full_step = jnp.concatenate([correction, pressure_step[None]], axis=0)
    smoothed = solution + full_step

    smoothed_masked = smoothed * active[None]
    sm_grid = smoothed_masked[:3].reshape(grid)
    edge = (3, 1, y_cells, LAYERS)
    x_low2 = x_low + near_corr[:, :1].reshape(edge)
    x_high2 = x_high + near_corr[:, -1:].reshape(edge)
    y_low2, y_high2 = neighbour_shift(sm_grid, "gy", 2, 1)
    in_cell2 = in_cell_terms(smoothed_masked, matrix)
    moving2 = in_cell2[:3] + neighbour_terms(sm_grid, x_low2, x_high2, y_low2, y_high2, viscosity, frozen)
    post = active[None] * (forcing - jnp.concatenate([moving2, in_cell2[3:]], axis=0))

    column_residual = jnp.sum(post.reshape(4, row_count, y_cells, LAYERS), axis=-1)
    basin_count = lax.axis_size("gx") // 2 * lax.axis_size("gy")
    member = basin_map.reshape(-1)[:, None] == jnp.arange(basin_count, dtype=jnp.int32)[None, :]
    partial_sums = jnp.sum(
        jnp.where(member[None], column_residual.reshape(4, -1)[:, :, None], 0.0), axis=1
    )
    basin_residual = tree_sum(tree_sum(partial_sums, "gx"), "gy")
    return (smoothed, column_residual, basin_residual)


def solution(mesh):
    return jax.shard_map(
        local,
        mesh=mesh,
        in_specs=(
            P(None, "gx", "gy"),
            P(None, "gx", "gy"),
            P("gx", "gy"),
            P(None, "gx", "gy"),
            P("gx", "gy"),
            P("gx", "gy"),
            P("gx", "gy"),
        ),
        out_specs=(P(None, "gx", "gy"), P(None, "gx", "gy"), P()),
        check_vma=False,
    )
```

time: 177 us -> 68 us (0.38)
  blocking collectives: 134 us -> 0 us
  starting transfers between devices: 14.8 us -> 29.6 us
  waiting for transfers between devices: 13.9 us -> 24.6 us
  other arithmetic: 4.04 us -> 7.07 us
  local copies, waits for them, and re-layouts: 7.38 us -> 4.98 us
    all_gather x3 -> x0, blocking collectives: 93.5 us -> none  [carried_in(): pieces = lax.all_gather(value, axis)]
    psum x1 -> x0, blocking collectives: 40.7 us -> none  [local(): basin_residual = lax.psum(partial_sums, ('gx', 'gy'))]
    ppermute x8 -> x18, starting transfers between devices: 14.8 us -> 29.6 us  [the longest x7 12.5 us: gather_rows(): pieces.append(lax.ppermute(block, axis, pairs))]
    ppermute x8 -> x18, waiting for transfers between devices: 13.9 us -> 24.6 us  [the longest x5 12.8 us: tree_sum(): lax.ppermute(value, axis, [(i, i ^ step) for i in range(count)])]
    unnamed x30 -> x25, local copies, waits for them, and re-layouts: 4.69 us -> 0.24 us
  transfers between devices with their start and end apart: 8 -> 18, of which waited for: 5 -> 8; matrix products, arithmetic and copies ran while one was open for 0% -> 6% of each run, Pallas kernels for 0% -> 0%
where the time goes in v1:
time: 68 us; the launch traced here: 67.5 us
  starting transfers between devices  29.6 us (44%)
  waiting for transfers between devices  24.6 us (36%)
  other arithmetic  7.07 us (10%)
  local copies, waits for them, and re-layouts  4.98 us (7%)
  between operations  1.19 us (2%)
    ppermute x5, waiting for transfers between devices, tree_sum(): lax.ppermute(value, axis, [(i, i ^ step) for i in range(count)])  12.8 us
    ppermute x7, starting transfers between devices, gather_rows(): pieces.append(lax.ppermute(block, axis, pairs))  12.5 us
    ppermute x3, starting transfers between devices, neighbour_shift(): lax.ppermute(lax.slice_in_dim(block, block.shape[dim] - width, None, axis...  9.4 us
    ppermute x7, waiting for transfers between devices, gather_rows(): pieces.append(lax.ppermute(block, axis, pairs))  8.35 us
    ppermute x3, starting transfers between devices, neighbour_shift(): lax.ppermute(lax.slice_in_dim(block, 0, width, axis=dim), axis, backward)  3.88 us
    ppermute x5, starting transfers between devices, tree_sum(): lax.ppermute(value, axis, [(i, i ^ step) for i in range(count)])  3.84 us
    ppermute x3, waiting for transfers between devices, neighbour_shift(): lax.ppermute(lax.slice_in_dim(block, 0, width, axis=dim), axis, backward)  3.43 us
  transfers between devices with their start and end apart: 18, of which 8 were waited for; matrix products, arithmetic and copies ran while one was open for 6% of the time, Pallas kernels for 0%

profile of v1, /device:TPU:0, one launch (start us, length us, event | category | flops | bytes accessed | tf_op | source)
XLA Modules:
  0.0 67.5 jit_solution(17125646122627989782)
XLA Ops:
  0.7 0.8 %lt.37 = s32[2,16,80]{2,1,0:T(8,128)S(1)} broadcast(s32[2,16]{1,0:T(2,128)} %param.11), dimensions={0,1} | broadcast | bytes 10368 | tf_op jit(solution)/shard_map/lt | solution.py:116
  1.4 0.1 lt.38
  1.5 0.1 lt.35
  1.6 0.8 %broadcast_multiply_fusion.1 = f32[1,8,1280]{2,1,0:T(8,128)S(1)} fusion(f32[1,8,1280]{2,1,0:T(8,128)} %bitcast.117, f32[8,1280]{1,0:T(8,128)S(1)} %bitcast.116), kind=kLoop, calls=%fused_computation.61 | loop fusion | flops 10240 | bytes 122880 | tf_op jit(solution)/shard_map/mul | solution.py:124
  2.4 0.1 reshape.154
  2.6 4.9 %collective-permute-start = (f32[3,1,16,80]{3,2,0,1:T(8,128)S(1)}, f32[3,1,16,80]{3,2,0,1:T(8,128)S(1)}, u32[]{:S(2)}, u32[]{:S(2)}) collective-permute-start(f32[3,1,16,80]{3,2,0,1:T(8,128)S(1)} %get-tuple-element.85), channel_id=1, source_target_pairs={{0,4},{4,8},{8,12},{12,16},{16,20},{20,24},{24,28},{1,5},{5,9},{9,... | collective-permute-start | bytes 46088 | tf_op jit(solution)/shard_map/ppermute | solution.py:16
  7.4 1.3 %collective-permute-start.1 = (f32[3,1,16,80]{3,2,0,1:T(8,128)S(1)}, f32[3,1,16,80]{3,2,0,1:T(8,128)S(1)}, u32[]{:S(2)}, u32[]{:S(2)}) collective-permute-start(f32[3,1,16,80]{3,2,0,1:T(8,128)S(1)} %get-tuple-element.86), channel_id=1, source_target_pairs={{4,0},{8,4},{12,8},{16,12},{20,16},{24,20},{28,24},{5,1},{9,5},{13... | collective-permute-start | bytes 46088 | tf_op jit(solution)/shard_map/ppermute | solution.py:17
  8.8 1.5 %collective-permute-start.2 = (f32[3,2,1,80]{3,2,1,0:T(1,128)S(1)}, f32[3,2,1,80]{3,2,1,0:T(1,128)S(1)}, u32[]{:S(2)}, u32[]{:S(2)}) collective-permute-start(f32[3,2,1,80]{3,2,1,0:T(1,128)S(1)} %get-tuple-element.89), channel_id=1, source_target_pairs={{0,1},{1,2},{2,3},{4,5},{5,6},{6,7},{8,9},{9,10},{10,11},{12,13},{... | collective-permute-start | bytes 5768 | tf_op jit(solution)/shard_map/ppermute | solution.py:16
  10.2 1.3 %collective-permute-start.3 = (f32[3,2,1,80]{3,2,1,0:T(1,128)S(1)}, f32[3,2,1,80]{3,2,1,0:T(1,128)S(1)}, u32[]{:S(2)}, u32[]{:S(2)}) collective-permute-start(f32[3,2,1,80]{3,2,1,0:T(1,128)S(1)} %get-tuple-element.90), channel_id=1, source_target_pairs={{1,0},{2,1},{3,2},{5,4},{6,5},{7,6},{9,8},{10,9},{11,10},{13,12},{... | collective-permute-start | bytes 5768 | tf_op jit(solution)/shard_map/ppermute | solution.py:17
  11.5 0.1 fusion.55
  11.6 0.7 %convert_subtract_fusion = f32[2,16]{1,0:T(2,128)S(1)} fusion(s32[2,16]{1,0:T(2,128)} %param.12), kind=kLoop, calls=%fused_computation.182 | loop fusion | flops 64 | bytes 256 | tf_op jit(solution)/shard_map/sub | solution.py:23
  12.3 0.1 slice_multiply_fusion.1
  12.4 0.7 %broadcast_multiply_fusion.3 = (f32[2,1280]{1,0:T(2,128)S(1)}, f32[1,2,1280]{2,1,0:T(2,128)S(1)}, f32[2,1280]{1,0:T(2,128)S(1)}) fusion(f32[2,1280]{1,0:T(2,128)} %param.9, pred[2,1280]{1,0:T(4,128)(4,1)S(1)} %get-tuple-element.71), kind=kLoop, calls=%fused_computation.178 | loop fusion | flops 7680 | bytes 43520 | tf_op jit(solution)/shard_map/mul | solution.py:133
  13.1 0.7 %slice_bitcast_fusion.8 = (f32[1,2,1280]{2,1,0:T(2,128)S(1)}, f32[1,2,1280]{2,1,0:T(2,128)S(1)}, f32[1,2,1280]{2,1,0:T(2,128)S(1)}) fusion(f32[4,4,2,1280]{3,2,1,0:T(2,128)} %bitcast.112), kind=kLoop, calls=%fused_computation.142 | loop fusion | bytes 61440 | tf_op jit(solution)/shard_map/stack;squeeze | solution.py:132
  13.8 0.8 %eq.19 = s32[32]{0:T(128)S(1)} reshape(s32[2,16]{1,0:T(2,128)} %param.13) | data formatting | bytes 256 | tf_op jit(solution)/shard_map/eq | solution.py:165
  14.6 1.0 %multiply_reduce_fusion.1 = f32[4,2,1280]{2,1,0:T(2,128)S(1)} fusion(f32[4,2,1280]{2,1,0:T(2,128)S(1)} %bitcast.115, f32[16,2,1280]{2,1,0:T(2,128)} %param.10), kind=kLoop, calls=%fused_computation.8 | loop fusion | flops 71680 | bytes 245760 | tf_op jit(solution)/shard_map/reduce_sum | solution.py:40
  15.7 0.1 fusion.6
  15.8 0.1 reshape.155
  15.9 0.1 reshape.156
  16.0 0.1 slice_add_fusion.1
  16.2 5.6 %collective-permute-start.4 = (f32[7,2,1280]{2,1,0:T(2,128)S(1)}, f32[7,2,1280]{2,1,0:T(2,128)S(1)}, u32[]{:S(2)}, u32[]{:S(2)}) collective-permute-start(f32[7,2,1280]{2,1,0:T(2,128)S(1)} %pad_maximum_fusion), channel_id=1, source_target_pairs={{4,0},{8,4},{12,8},{16,12},{20,16},{24,20},{28,24},{0,28},{5,1},{9... | collective-permute-start | bytes 215048 | tf_op jit(solution)/shard_map/ppermute | solution.py:50
  21.8 0.5 collective-permute-start.5
  22.3 0.4 collective-permute-start.6
  22.7 3.5 %collective-permute-start.7 = (f32[7,2,1280]{2,1,0:T(2,128)S(1)}, f32[7,2,1280]{2,1,0:T(2,128)S(1)}, u32[]{:S(2)}, u32[]{:S(2)}) collective-permute-start(f32[7,2,1280]{2,1,0:T(2,128)S(1)} %pad_maximum_fusion), channel_id=1, source_target_pairs={{16,0},{20,4},{24,8},{28,12},{0,16},{4,20},{8,24},{12,28},{17,1},{... | collective-permute-start | bytes 215048 | tf_op jit(solution)/shard_map/ppermute | solution.py:50
  26.2 0.9 %collective-permute-start.9 = (f32[7,2,1280]{2,1,0:T(2,128)S(1)}, f32[7,2,1280]{2,1,0:T(2,128)S(1)}, u32[]{:S(2)}, u32[]{:S(2)}) collective-permute-start(f32[7,2,1280]{2,1,0:T(2,128)S(1)} %pad_maximum_fusion), channel_id=1, source_target_pairs={{24,0},{28,4},{0,8},{4,12},{8,16},{12,20},{16,24},{20,28},{25,1},{... | collective-permute-start | bytes 215048 | tf_op jit(solution)/shard_map/ppermute | solution.py:50
  27.1 1.6 %collective-permute-start.10 = (f32[7,2,1280]{2,1,0:T(2,128)S(1)}, f32[7,2,1280]{2,1,0:T(2,128)S(1)}, u32[]{:S(2)}, u32[]{:S(2)}) collective-permute-start(f32[7,2,1280]{2,1,0:T(2,128)S(1)} %pad_maximum_fusion), channel_id=1, source_target_pairs={{28,0},{0,4},{4,8},{8,12},{12,16},{16,20},{20,24},{24,28},{29,1},{... | collective-permute-start | bytes 215048 | tf_op jit(solution)/shard_map/ppermute | solution.py:50
  28.8 7.1 %collective-permute-done.7 = f32[7,2,1280]{2,1,0:T(2,128)S(1)} collective-permute-done((f32[7,2,1280]{2,1,0:T(2,128)S(1)}, f32[7,2,1280]{2,1,0:T(2,128)S(1)}, u32[]{:S(2)}, u32[]{:S(2)}) %collective-permute-start.7) | collective-permute-done | bytes 71712 | tf_op jit(solution)/shard_map/ppermute | solution.py:50
  35.9 1.2 %collective-permute-done.8 = f32[7,2,1280]{2,1,0:T(2,128)S(1)} collective-permute-done((f32[7,2,1280]{2,1,0:T(2,128)S(1)}, f32[7,2,1280]{2,1,0:T(2,128)S(1)}, u32[]{:S(2)}, u32[]{:S(2)}) %collective-permute-start.8) | collective-permute-done | bytes 71712 | tf_op jit(solution)/shard_map/ppermute | solution.py:50
  37.4 0.1 dynamic-slice_bitcast_fusion
  37.6 0.2 slice.363
  37.8 0.1 broadcast_in_dim.95
  37.8 0.2 slice_reduce_fusion
  38.1 0.2 slice.358
  38.3 0.4 broadcast_divide_fusion
  38.7 0.6 fusion.14
  39.4 0.4 multiply_add_fusion
  39.7 0.4 stack.32
  40.2 0.1 fusion.37
  40.2 0.7 broadcast_multiply_fusion
  40.9 0.1 reshape.157
  41.0 0.1 fusion.53
  41.1 0.1 slice_multiply_fusion
  41.2 0.1 fusion.12
  41.3 0.1 reshape.158
  41.4 0.1 reshape.159
  41.5 3.1 %collective-permute-start.11 = (f32[3,2,1,80]{3,2,1,0:T(1,128)S(1)}, f32[3,2,1,80]{3,2,1,0:T(1,128)S(1)}, u32[]{:S(2)}, u32[]{:S(2)}) collective-permute-start(f32[3,2,1,80]{3,2,1,0:T(1,128)S(1)} %get-tuple-element.81), channel_id=1, source_target_pairs={{0,1},{1,2},{2,3},{4,5},{5,6},{6,7},{8,9},{9,10},{10,11},{12,13},{... | collective-permute-start | bytes 5768 | tf_op jit(solution)/shard_map/ppermute | solution.py:16
  44.6 1.3 %collective-permute-start.12 = (f32[3,2,1,80]{3,2,1,0:T(1,128)S(1)}, f32[3,2,1,80]{3,2,1,0:T(1,128)S(1)}, u32[]{:S(2)}, u32[]{:S(2)}) collective-permute-start(f32[3,2,1,80]{3,2,1,0:T(1,128)S(1)} %get-tuple-element.82), channel_id=1, source_target_pairs={{1,0},{2,1},{3,2},{5,4},{6,5},{7,6},{9,8},{10,9},{11,10},{13,12},{... | collective-permute-start | bytes 5768 | tf_op jit(solution)/shard_map/ppermute | solution.py:17
  45.9 0.1 multiply_reduce_fusion
  46.0 3.4 %collective-permute-done.12 = f32[3,2,1,80]{3,2,1,0:T(1,128)S(1)} collective-permute-done((f32[3,2,1,80]{3,2,1,0:T(1,128)S(1)}, f32[3,2,1,80]{3,2,1,0:T(1,128)S(1)}, u32[]{:S(2)}, u32[]{:S(2)}) %collective-permute-start.12) | collective-permute-done | bytes 1952 | tf_op jit(solution)/shard_map/ppermute | solution.py:17
  49.4 0.1 fusion.2
  49.5 0.1 reshape.160
  49.6 0.1 reshape.161
  49.8 0.1 reshape.162
  49.9 0.1 reduce_sum.38
  50.0 0.1 broadcast_in_dim.115
  50.1 0.1 select_reduce_fusion
  50.2 3.6 %collective-permute-done.13 = f32[4,16]{1,0:T(4,128)S(1)} collective-permute-done((f32[4,16]{1,0:T(4,128)S(1)}, f32[4,16]{1,0:T(4,128)S(1)}, u32[]{:S(2)}, u32[]{:S(2)}) %collective-permute-start.13) | collective-permute-done | bytes 288 | tf_op jit(solution)/shard_map/ppermute | solution.py:105
  53.8 3.6 %collective-permute-done.14 = f32[4,16]{1,0:T(4,128)S(1)} collective-permute-done((f32[4,16]{1,0:T(4,128)S(1)}, f32[4,16]{1,0:T(4,128)S(1)}, u32[]{:S(2)}, u32[]{:S(2)}) %collective-permute-start.14) | collective-permute-done | bytes 288 | tf_op jit(solution)/shard_map/ppermute | solution.py:105
  57.4 1.6 %collective-permute-start.15 = (f32[4,16]{1,0:T(4,128)S(1)}, f32[4,16]{1,0:T(4,128)S(1)}, u32[]{:S(2)}, u32[]{:S(2)}) collective-permute-start(f32[4,16]{1,0:T(4,128)S(1)} %add.613), channel_id=1, source_target_pairs={{0,16},{4,20},{8,24},{12,28},{16,0},{20,4},{24,8},{28,12},{1,17},{... | collective-permute-start | bytes 776 | tf_op jit(solution)/shard_map/ppermute | solution.py:105
  59.0 2.9 %collective-permute-done.15 = f32[4,16]{1,0:T(4,128)S(1)} collective-permute-done((f32[4,16]{1,0:T(4,128)S(1)}, f32[4,16]{1,0:T(4,128)S(1)}, u32[]{:S(2)}, u32[]{:S(2)}) %collective-permute-start.15) | collective-permute-done | bytes 288 | tf_op jit(solution)/shard_map/ppermute | solution.py:105
  61.9 1.2 %collective-permute-done.16 = f32[4,16]{1,0:T(4,128)S(1)} collective-permute-done((f32[4,16]{1,0:T(4,128)S(1)}, f32[4,16]{1,0:T(4,128)S(1)}, u32[]{:S(2)}, u32[]{:S(2)}) %collective-permute-start.16) | collective-permute-done | bytes 288 | tf_op jit(solution)/shard_map/ppermute | solution.py:105
  63.1 2.3 %collective-permute-start.17 = (f32[4,16]{1,0:T(4,128)S(1)}, f32[4,16]{1,0:T(4,128)S(1)}, u32[]{:S(2)}, u32[]{:S(2)}) collective-permute-start(f32[4,16]{1,0:T(4,128)S(1)} %add.615), channel_id=1, source_target_pairs={{0,2},{1,3},{2,0},{3,1},{4,6},{5,7},{6,4},{7,5},{8,10},{9,11},{10,... | collective-permute-start | bytes 776 | tf_op jit(solution)/shard_map/ppermute | solution.py:105
  65.3 1.6 %collective-permute-done.17 = f32[4,16]{1,0:T(4,128)S(1)} collective-permute-done((f32[4,16]{1,0:T(4,128)S(1)}, f32[4,16]{1,0:T(4,128)S(1)}, u32[]{:S(2)}, u32[]{:S(2)}) %collective-permute-start.17) | collective-permute-done | bytes 288 | tf_op jit(solution)/shard_map/ppermute | solution.py:105
  66.9 0.6 add.616
  (68 shorter events, 0.7 us)
Async XLA Ops:
  0.6 15.4 %copy-start.1 = (f32[2,1280]{1,0:T(2,128)S(1)}, f32[2,1280]{1,0:T(2,128)}, u32[]{:S(2)}) copy-start(f32[2,1280]{1,0:T(2,128)} %param.9) | copy-start | bytes 30724
  0.6 15.4 %copy-start.2 = (f32[4,2,1280]{2,1,0:T(2,128)S(1)}, f32[4,2,1280]{2,1,0:T(2,128)}, u32[]{:S(2)}) copy-start(f32[4,2,1280]{2,1,0:T(2,128)} %param.8) | copy-start | bytes 122884
  2.6 13.1 %collective-permute-start = (f32[3,1,16,80]{3,2,0,1:T(8,128)S(1)}, f32[3,1,16,80]{3,2,0,1:T(8,128)S(1)}, u32[]{:S(2)}, u32[]{:S(2)}) collective-permute-start(f32[3,1,16,80]{3,2,0,1:T(8,128)S(1)} %get-tuple-element.85), channel_id=1, source_target_pairs={{0,4},{4,8},{8,12},{12,16},{16,20},{20,24},{24,28},{1,5},{5,9},{9,... | collective-permute-start | bytes 46088 | tf_op jit(solution)/shard_map/ppermute | solution.py:16
  7.4 8.2 %collective-permute-start.1 = (f32[3,1,16,80]{3,2,0,1:T(8,128)S(1)}, f32[3,1,16,80]{3,2,0,1:T(8,128)S(1)}, u32[]{:S(2)}, u32[]{:S(2)}) collective-permute-start(f32[3,1,16,80]{3,2,0,1:T(8,128)S(1)} %get-tuple-element.86), channel_id=1, source_target_pairs={{4,0},{8,4},{12,8},{16,12},{20,16},{24,20},{28,24},{5,1},{9,5},{13... | collective-permute-start | bytes 46088 | tf_op jit(solution)/shard_map/ppermute | solution.py:17
  8.8 6.9 %collective-permute-start.2 = (f32[3,2,1,80]{3,2,1,0:T(1,128)S(1)}, f32[3,2,1,80]{3,2,1,0:T(1,128)S(1)}, u32[]{:S(2)}, u32[]{:S(2)}) collective-permute-start(f32[3,2,1,80]{3,2,1,0:T(1,128)S(1)} %get-tuple-element.89), channel_id=1, source_target_pairs={{0,1},{1,2},{2,3},{4,5},{5,6},{6,7},{8,9},{9,10},{10,11},{12,13},{... | collective-permute-start | bytes 5768 | tf_op jit(solution)/shard_map/ppermute | solution.py:16
  10.2 5.4 %collective-permute-start.3 = (f32[3,2,1,80]{3,2,1,0:T(1,128)S(1)}, f32[3,2,1,80]{3,2,1,0:T(1,128)S(1)}, u32[]{:S(2)}, u32[]{:S(2)}) collective-permute-start(f32[3,2,1,80]{3,2,1,0:T(1,128)S(1)} %get-tuple-element.90), channel_id=1, source_target_pairs={{1,0},{2,1},{3,2},{5,4},{6,5},{7,6},{9,8},{10,9},{11,10},{13,12},{... | collective-permute-start | bytes 5768 | tf_op jit(solution)/shard_map/ppermute | solution.py:17
  16.2 10.0 %collective-permute-start.4 = (f32[7,2,1280]{2,1,0:T(2,128)S(1)}, f32[7,2,1280]{2,1,0:T(2,128)S(1)}, u32[]{:S(2)}, u32[]{:S(2)}) collective-permute-start(f32[7,2,1280]{2,1,0:T(2,128)S(1)} %pad_maximum_fusion), channel_id=1, source_target_pairs={{4,0},{8,4},{12,8},{16,12},{20,16},{24,20},{28,24},{0,28},{5,1},{9... | collective-permute-start | bytes 215048 | tf_op jit(solution)/shard_map/ppermute | solution.py:50
  21.8 5.4 %collective-permute-start.5 = (f32[7,2,1280]{2,1,0:T(2,128)S(1)}, f32[7,2,1280]{2,1,0:T(2,128)S(1)}, u32[]{:S(2)}, u32[]{:S(2)}) collective-permute-start(f32[7,2,1280]{2,1,0:T(2,128)S(1)} %pad_maximum_fusion), channel_id=1, source_target_pairs={{8,0},{12,4},{16,8},{20,12},{24,16},{28,20},{0,24},{4,28},{9,1},{1... | collective-permute-start | bytes 215048 | tf_op jit(solution)/shard_map/ppermute | solution.py:50
  22.3 6.5 %collective-permute-start.6 = (f32[7,2,1280]{2,1,0:T(2,128)S(1)}, f32[7,2,1280]{2,1,0:T(2,128)S(1)}, u32[]{:S(2)}, u32[]{:S(2)}) collective-permute-start(f32[7,2,1280]{2,1,0:T(2,128)S(1)} %pad_maximum_fusion), channel_id=1, source_target_pairs={{12,0},{16,4},{20,8},{24,12},{28,16},{0,20},{4,24},{8,28},{13,1},{... | collective-permute-start | bytes 215048 | tf_op jit(solution)/shard_map/ppermute | solution.py:50
  22.7 13.2 %collective-permute-start.7 = (f32[7,2,1280]{2,1,0:T(2,128)S(1)}, f32[7,2,1280]{2,1,0:T(2,128)S(1)}, u32[]{:S(2)}, u32[]{:S(2)}) collective-permute-start(f32[7,2,1280]{2,1,0:T(2,128)S(1)} %pad_maximum_fusion), channel_id=1, source_target_pairs={{16,0},{20,4},{24,8},{28,12},{0,16},{4,20},{8,24},{12,28},{17,1},{... | collective-permute-start | bytes 215048 | tf_op jit(solution)/shard_map/ppermute | solution.py:50
  26.2 11.0 %collective-permute-start.8 = (f32[7,2,1280]{2,1,0:T(2,128)S(1)}, f32[7,2,1280]{2,1,0:T(2,128)S(1)}, u32[]{:S(2)}, u32[]{:S(2)}) collective-permute-start(f32[7,2,1280]{2,1,0:T(2,128)S(1)} %pad_maximum_fusion), channel_id=1, source_target_pairs={{20,0},{24,4},{28,8},{0,12},{4,16},{8,20},{12,24},{16,28},{21,1},{... | collective-permute-start | bytes 215048 | tf_op jit(solution)/shard_map/ppermute | solution.py:50
  26.2 11.0 %collective-permute-start.9 = (f32[7,2,1280]{2,1,0:T(2,128)S(1)}, f32[7,2,1280]{2,1,0:T(2,128)S(1)}, u32[]{:S(2)}, u32[]{:S(2)}) collective-permute-start(f32[7,2,1280]{2,1,0:T(2,128)S(1)} %pad_maximum_fusion), channel_id=1, source_target_pairs={{24,0},{28,4},{0,8},{4,12},{8,16},{12,20},{16,24},{20,28},{25,1},{... | collective-permute-start | bytes 215048 | tf_op jit(solution)/shard_map/ppermute | solution.py:50
  27.1 10.1 %collective-permute-start.10 = (f32[7,2,1280]{2,1,0:T(2,128)S(1)}, f32[7,2,1280]{2,1,0:T(2,128)S(1)}, u32[]{:S(2)}, u32[]{:S(2)}) collective-permute-start(f32[7,2,1280]{2,1,0:T(2,128)S(1)} %pad_maximum_fusion), channel_id=1, source_target_pairs={{28,0},{0,4},{4,8},{8,12},{12,16},{16,20},{20,24},{24,28},{29,1},{... | collective-permute-start | bytes 215048 | tf_op jit(solution)/shard_map/ppermute | solution.py:50
  38.7 1.4 %copy-start = (f32[16,2,1280]{2,1,0:T(2,128)S(1)}, f32[16,2,1280]{2,1,0:T(2,128)}, u32[]{:S(2)}) copy-start(f32[16,2,1280]{2,1,0:T(2,128)} %param.10) | copy-start | bytes 491524
  39.4 0.9 %copy-start.3 = (f32[4,2,1280]{2,1,0:T(2,128)S(1)}, f32[4,2,1280]{2,1,0:T(2,128)}, u32[]{:S(2)}) copy-start(f32[4,2,1280]{2,1,0:T(2,128)} %param.7) | copy-start | bytes 122884
  41.5 4.5 %collective-permute-start.11 = (f32[3,2,1,80]{3,2,1,0:T(1,128)S(1)}, f32[3,2,1,80]{3,2,1,0:T(1,128)S(1)}, u32[]{:S(2)}, u32[]{:S(2)}) collective-permute-start(f32[3,2,1,80]{3,2,1,0:T(1,128)S(1)} %get-tuple-element.81), channel_id=1, source_target_pairs={{0,1},{1,2},{2,3},{4,5},{5,6},{6,7},{8,9},{9,10},{10,11},{12,13},{... | collective-permute-start | bytes 5768 | tf_op jit(solution)/shard_map/ppermute | solution.py:16
  44.6 4.9 %collective-permute-start.12 = (f32[3,2,1,80]{3,2,1,0:T(1,128)S(1)}, f32[3,2,1,80]{3,2,1,0:T(1,128)S(1)}, u32[]{:S(2)}, u32[]{:S(2)}) collective-permute-start(f32[3,2,1,80]{3,2,1,0:T(1,128)S(1)} %get-tuple-element.82), channel_id=1, source_target_pairs={{1,0},{2,1},{3,2},{5,4},{6,5},{7,6},{9,8},{10,9},{11,10},{13,12},{... | collective-permute-start | bytes 5768 | tf_op jit(solution)/shard_map/ppermute | solution.py:17
  50.0 17.5 %copy-start.4 = (f32[4,2,16]{2,1,0:T(2,128)}, f32[4,2,16]{2,1,0:T(2,128)S(1)}, u32[]{:S(2)}) copy-start(f32[4,2,16]{2,1,0:T(2,128)S(1)} %reduce_sum.38) | copy-start | bytes 1540
  50.2 3.6 %collective-permute-start.13 = (f32[4,16]{1,0:T(4,128)S(1)}, f32[4,16]{1,0:T(4,128)S(1)}, u32[]{:S(2)}, u32[]{:S(2)}) collective-permute-start(f32[4,16]{1,0:T(4,128)S(1)} %select_reduce_fusion), channel_id=1, source_target_pairs={{0,4},{4,0},{8,12},{12,8},{16,20},{20,16},{24,28},{28,24},{1,5},{5... | collective-permute-start | bytes 776 | tf_op jit(solution)/shard_map/ppermute | solution.py:105
  53.8 3.6 %collective-permute-start.14 = (f32[4,16]{1,0:T(4,128)S(1)}, f32[4,16]{1,0:T(4,128)S(1)}, u32[]{:S(2)}, u32[]{:S(2)}) collective-permute-start(f32[4,16]{1,0:T(4,128)S(1)} %add.612), channel_id=1, source_target_pairs={{0,8},{4,12},{8,0},{12,4},{16,24},{20,28},{24,16},{28,20},{1,9},{5... | collective-permute-start | bytes 776 | tf_op jit(solution)/shard_map/ppermute | solution.py:105
  57.4 4.5 %collective-permute-start.15 = (f32[4,16]{1,0:T(4,128)S(1)}, f32[4,16]{1,0:T(4,128)S(1)}, u32[]{:S(2)}, u32[]{:S(2)}) collective-permute-start(f32[4,16]{1,0:T(4,128)S(1)} %add.613), channel_id=1, source_target_pairs={{0,16},{4,20},{8,24},{12,28},{16,0},{20,4},{24,8},{28,12},{1,17},{... | collective-permute-start | bytes 776 | tf_op jit(solution)/shard_map/ppermute | solution.py:105
  61.9 1.2 %collective-permute-start.16 = (f32[4,16]{1,0:T(4,128)S(1)}, f32[4,16]{1,0:T(4,128)S(1)}, u32[]{:S(2)}, u32[]{:S(2)}) collective-permute-start(f32[4,16]{1,0:T(4,128)S(1)} %add.614), channel_id=1, source_target_pairs={{0,1},{1,0},{2,3},{3,2},{4,5},{5,4},{6,7},{7,6},{8,9},{9,8},{10,11... | collective-permute-start | bytes 776 | tf_op jit(solution)/shard_map/ppermute | solution.py:105
  63.1 3.8 %collective-permute-start.17 = (f32[4,16]{1,0:T(4,128)S(1)}, f32[4,16]{1,0:T(4,128)S(1)}, u32[]{:S(2)}, u32[]{:S(2)}) collective-permute-start(f32[4,16]{1,0:T(4,128)S(1)} %add.615), channel_id=1, source_target_pairs={{0,2},{1,3},{2,0},{3,1},{4,6},{5,7},{6,4},{7,5},{8,10},{9,11},{10,... | collective-permute-start | bytes 776 | tf_op jit(solution)/shard_map/ppermute | solution.py:105

commit v2 on v1

--- a/solution.py
+++ b/solution.py
@@ -121,6 +121,9 @@
     matrix = blocks.reshape(4, 4, row_count, lane_count)
     grid = (3, row_count, y_cells, LAYERS)
 
+    diagonal = jnp.stack([matrix[0, 0], matrix[1, 1], matrix[2, 2]])
+    line_lead = jnp.where(active[None] > 0.0, diagonal + 2.0 * viscosity[None], 1.0)
+    line_off = (viscosity * active)[None]
     masked = solution * active[None]
     masked_grid = masked[:3].reshape(grid)
     x_low, x_high = neighbour_shift(masked_grid, "gx", 1, 1)
@@ -129,14 +132,12 @@
     moving = in_cell[:3] + neighbour_terms(masked_grid, x_low, x_high, y_low, y_high, viscosity, frozen)
     residual = active[None] * (forcing - jnp.concatenate([moving, in_cell[3:]], axis=0))
 
-    diagonal = jnp.stack([matrix[0, 0], matrix[1, 1], matrix[2, 2]])
-    line_lead = jnp.where(active[None] > 0.0, diagonal + 2.0 * viscosity[None], 1.0)
-    line_off = (viscosity * active)[None]
-    packed = jnp.concatenate([line_lead, line_off, residual[:3]], axis=0)
-    whole = gather_rows(packed, "gx")
-    all_rows = whole.shape[1]
+    whole_coef = gather_rows(jnp.concatenate([line_lead, line_off], axis=0), "gx")
+    whole_rhs = gather_rows(residual[:3], "gx")
+    all_rows = whole_rhs.shape[1]
     solver = line_solve if all_rows <= 32 else line_solve_scan
-    whole_corr = solver(whole[0:3], jnp.broadcast_to(whole[3:4], (3,) + whole.shape[1:]), whole[4:7])
+    whole_off = jnp.broadcast_to(whole_coef[3:4], (3,) + whole_rhs.shape[1:])
+    whole_corr = solver(whole_coef[0:3], whole_off, whole_rhs)
 
     first = lax.axis_index("gx") * row_count
     padded_corr = jnp.pad(whole_corr, ((0, 0), (1, 1), (0, 0)))

time: 68 us -> 77.6 us (1.14)
  starting transfers between devices: 29.6 us -> 40.5 us
  local copies, waits for them, and re-layouts: 4.98 us -> 8.76 us
  other arithmetic: 7.07 us -> 3.91 us
  waiting for transfers between devices: 24.6 us -> 22.6 us
    ppermute x7 -> x14, starting transfers between devices: 12.5 us -> 28.4 us  [gather_rows(): pieces.append(lax.ppermute(block, axis, pairs))]
    ppermute x3, starting transfers between devices: 9.4 us -> 4.03 us  [neighbour_shift(): lax.ppermute(lax.slice_in_dim(block, block.shape[dim] - width, None, axis...]
    unnamed x25 -> x46, local copies, waits for them, and re-layouts: 0.24 us -> 4.03 us
    ppermute x7 -> x14, waiting for transfers between devices: 8.35 us -> 5.1 us  [gather_rows(): pieces.append(lax.ppermute(block, axis, pairs))]
    ppermute x3, waiting for transfers between devices: 3.43 us -> 5.05 us  [neighbour_shift(): lax.ppermute(lax.slice_in_dim(block, 0, width, axis=dim), axis, backward)]
    reduce_sum x2, other arithmetic: 1.09 us -> 0.15 us  [in_cell_terms(): return jnp.sum(matrix * masked[None], axis=1)]
    mul x1, other arithmetic: 0.79 us -> 0.01 us  [local(): masked = solution * active[None]]
  transfers between devices with their start and end apart: 18 -> 25, of which waited for: 8 -> 8; matrix products, arithmetic and copies ran while one was open for 6% -> 3% of each run, Pallas kernels for 0% -> 0%
where the time goes in v2:
time: 77.6 us; the launch traced here: 77.1 us
  starting transfers between devices  40.5 us (52%)
  waiting for transfers between devices  22.6 us (29%)
  local copies, waits for them, and re-layouts  8.76 us (11%)
  other arithmetic  3.91 us (5%)
  between operations  1.27 us (2%)
    ppermute x14, starting transfers between devices, gather_rows(): pieces.append(lax.ppermute(block, axis, pairs))  28.4 us
    ppermute x5, waiting for transfers between devices, tree_sum(): lax.ppermute(value, axis, [(i, i ^ step) for i in range(count)])  12.5 us
    ppermute x14, waiting for transfers between devices, gather_rows(): pieces.append(lax.ppermute(block, axis, pairs))  5.1 us
    ppermute x3, waiting for transfers between devices, neighbour_shift(): lax.ppermute(lax.slice_in_dim(block, 0, width, axis=dim), axis, backward)  5.05 us
    ppermute x5, starting transfers between devices, tree_sum(): lax.ppermute(value, axis, [(i, i ^ step) for i in range(count)])  4.18 us
    unnamed x46, local copies, waits for them, and re-layouts  4.03 us
    ppermute x3, starting transfers between devices, neighbour_shift(): lax.ppermute(lax.slice_in_dim(block, block.shape[dim] - width, None, axis...  4.03 us
    ppermute x3, starting transfers between devices, neighbour_shift(): lax.ppermute(lax.slice_in_dim(block, 0, width, axis=dim), axis, backward)  3.88 us
  transfers between devices with their start and end apart: 25, of which 8 were waited for; matrix products, arithmetic and copies ran while one was open for 3% of the time, Pallas kernels for 0%

profile of v2, /device:TPU:0, one launch (start us, length us, event | category | flops | bytes accessed | tf_op | source)
XLA Modules:
  0.0 77.1 jit_solution(2412244661706487176)
XLA Ops:
  0.6 0.7 lt.38
  1.4 0.1 lt.39
  1.6 0.7 slice_bitcast_fusion.8
  2.3 0.7 copy-done.2
  3.1 6.1 %collective-permute-start.11 = (f32[4,2,1280]{2,1,0:T(2,128)S(1)}, f32[4,2,1280]{2,1,0:T(2,128)S(1)}, u32[]{:S(2)}, u32[]{:S(2)}) collective-permute-start(f32[4,2,1280]{2,1,0:T(2,128)S(1)} %pad_maximum_fusion.8), channel_id=1, source_target_pairs={{4,0},{8,4},{12,8},{16,12},{20,16},{24,20},{28,24},{0,28},{5,1},{9... | collective-permute-start | bytes 122888 | tf_op jit(solution)/shard_map/ppermute | solution.py:50
  9.2 0.1 reshape.156
  9.3 1.3 %collective-permute-start = (f32[3,1,16,80]{3,2,0,1:T(8,128)S(1)}, f32[3,1,16,80]{3,2,0,1:T(8,128)S(1)}, u32[]{:S(2)}, u32[]{:S(2)}) collective-permute-start(f32[3,1,16,80]{3,2,0,1:T(8,128)S(1)} %get-tuple-element.83), channel_id=1, source_target_pairs={{0,4},{4,8},{8,12},{12,16},{16,20},{20,24},{24,28},{1,5},{5,9},{9,... | collective-permute-start | bytes 46088 | tf_op jit(solution)/shard_map/ppermute | solution.py:16
  10.6 1.3 %collective-permute-start.1 = (f32[3,1,16,80]{3,2,0,1:T(8,128)S(1)}, f32[3,1,16,80]{3,2,0,1:T(8,128)S(1)}, u32[]{:S(2)}, u32[]{:S(2)}) collective-permute-start(f32[3,1,16,80]{3,2,0,1:T(8,128)S(1)} %get-tuple-element.84), channel_id=1, source_target_pairs={{4,0},{8,4},{12,8},{16,12},{20,16},{24,20},{28,24},{5,1},{9,5},{13... | collective-permute-start | bytes 46088 | tf_op jit(solution)/shard_map/ppermute | solution.py:17
  11.9 1.5 %collective-permute-start.2 = (f32[3,2,1,80]{3,2,1,0:T(1,128)S(1)}, f32[3,2,1,80]{3,2,1,0:T(1,128)S(1)}, u32[]{:S(2)}, u32[]{:S(2)}) collective-permute-start(f32[3,2,1,80]{3,2,1,0:T(1,128)S(1)} %get-tuple-element.87), channel_id=1, source_target_pairs={{0,1},{1,2},{2,3},{4,5},{5,6},{6,7},{8,9},{9,10},{10,11},{12,13},{... | collective-permute-start | bytes 5768 | tf_op jit(solution)/shard_map/ppermute | solution.py:16
  13.4 1.3 %collective-permute-start.3 = (f32[3,2,1,80]{3,2,1,0:T(1,128)S(1)}, f32[3,2,1,80]{3,2,1,0:T(1,128)S(1)}, u32[]{:S(2)}, u32[]{:S(2)}) collective-permute-start(f32[3,2,1,80]{3,2,1,0:T(1,128)S(1)} %get-tuple-element.88), channel_id=1, source_target_pairs={{1,0},{2,1},{3,2},{5,4},{6,5},{7,6},{9,8},{10,9},{11,10},{13,12},{... | collective-permute-start | bytes 5768 | tf_op jit(solution)/shard_map/ppermute | solution.py:17
  14.8 0.1 fusion.54
  14.8 0.6 copy-done.6
  15.5 0.6 copy-done.7
  16.1 0.1 eq.19
  16.3 4.5 %collective-permute-start.12 = (f32[4,2,1280]{2,1,0:T(2,128)S(1)}, f32[4,2,1280]{2,1,0:T(2,128)S(1)}, u32[]{:S(2)}, u32[]{:S(2)}) collective-permute-start(f32[4,2,1280]{2,1,0:T(2,128)S(1)} %pad_maximum_fusion.8), channel_id=1, source_target_pairs={{8,0},{12,4},{16,8},{20,12},{24,16},{28,20},{0,24},{4,28},{9,1},{1... | collective-permute-start | bytes 122888 | tf_op jit(solution)/shard_map/ppermute | solution.py:50
  20.8 0.4 collective-permute-start.13
  21.2 1.8 %collective-permute-start.14 = (f32[4,2,1280]{2,1,0:T(2,128)S(1)}, f32[4,2,1280]{2,1,0:T(2,128)S(1)}, u32[]{:S(2)}, u32[]{:S(2)}) collective-permute-start(f32[4,2,1280]{2,1,0:T(2,128)S(1)} %pad_maximum_fusion.8), channel_id=1, source_target_pairs={{16,0},{20,4},{24,8},{28,12},{0,16},{4,20},{8,24},{12,28},{17,1},{... | collective-permute-start | bytes 122888 | tf_op jit(solution)/shard_map/ppermute | solution.py:50
  23.1 1.5 %collective-permute-start.15 = (f32[4,2,1280]{2,1,0:T(2,128)S(1)}, f32[4,2,1280]{2,1,0:T(2,128)S(1)}, u32[]{:S(2)}, u32[]{:S(2)}) collective-permute-start(f32[4,2,1280]{2,1,0:T(2,128)S(1)} %pad_maximum_fusion.8), channel_id=1, source_target_pairs={{20,0},{24,4},{28,8},{0,12},{4,16},{8,20},{12,24},{16,28},{21,1},{... | collective-permute-start | bytes 122888 | tf_op jit(solution)/shard_map/ppermute | solution.py:50
  24.6 0.1 fusion.6
  24.7 0.1 reshape.157
  24.8 0.1 reshape.158
  24.9 0.7 copy-done.3
  25.7 2.5 %collective-permute-start.16 = (f32[4,2,1280]{2,1,0:T(2,128)S(1)}, f32[4,2,1280]{2,1,0:T(2,128)S(1)}, u32[]{:S(2)}, u32[]{:S(2)}) collective-permute-start(f32[4,2,1280]{2,1,0:T(2,128)S(1)} %pad_maximum_fusion.8), channel_id=1, source_target_pairs={{24,0},{28,4},{0,8},{4,12},{8,16},{12,20},{16,24},{20,28},{25,1},{... | collective-permute-start | bytes 122888 | tf_op jit(solution)/shard_map/ppermute | solution.py:50
  28.4 4.8 %collective-permute-start.4 = (f32[3,2,1280]{2,1,0:T(2,128)S(1)}, f32[3,2,1280]{2,1,0:T(2,128)S(1)}, u32[]{:S(2)}, u32[]{:S(2)}) collective-permute-start(f32[3,2,1280]{2,1,0:T(2,128)S(1)} %slice.450), channel_id=1, source_target_pairs={{4,0},{8,4},{12,8},{16,12},{20,16},{24,20},{28,24},{0,28},{5,1},{9... | collective-permute-start | bytes 92168 | tf_op jit(solution)/shard_map/ppermute | solution.py:50
  33.4 3.0 %collective-permute-start.7 = (f32[3,2,1280]{2,1,0:T(2,128)S(1)}, f32[3,2,1280]{2,1,0:T(2,128)S(1)}, u32[]{:S(2)}, u32[]{:S(2)}) collective-permute-start(f32[3,2,1280]{2,1,0:T(2,128)S(1)} %slice.450), channel_id=1, source_target_pairs={{16,0},{20,4},{24,8},{28,12},{0,16},{4,20},{8,24},{12,28},{17,1},{... | collective-permute-start | bytes 92168 | tf_op jit(solution)/shard_map/ppermute | solution.py:50
  36.7 0.7 copy-done
  37.4 0.2 slice.355
  37.6 0.7 slice-done
  38.3 0.2 slice_reduce_fusion
  38.6 0.4 broadcast_divide_fusion
  39.0 2.1 %collective-permute-start.9 = (f32[3,2,1280]{2,1,0:T(2,128)S(1)}, f32[3,2,1280]{2,1,0:T(2,128)S(1)}, u32[]{:S(2)}, u32[]{:S(2)}) collective-permute-start(f32[3,2,1280]{2,1,0:T(2,128)S(1)} %slice.450), channel_id=1, source_target_pairs={{24,0},{28,4},{0,8},{4,12},{8,16},{12,20},{16,24},{20,28},{25,1},{... | collective-permute-start | bytes 92168 | tf_op jit(solution)/shard_map/ppermute | solution.py:50
  41.1 1.5 %collective-permute-start.10 = (f32[3,2,1280]{2,1,0:T(2,128)S(1)}, f32[3,2,1280]{2,1,0:T(2,128)S(1)}, u32[]{:S(2)}, u32[]{:S(2)}) collective-permute-start(f32[3,2,1280]{2,1,0:T(2,128)S(1)} %slice.450), channel_id=1, source_target_pairs={{28,0},{0,4},{4,8},{8,12},{12,16},{16,20},{20,24},{24,28},{29,1},{... | collective-permute-start | bytes 92168 | tf_op jit(solution)/shard_map/ppermute | solution.py:50
  42.7 3.5 %collective-permute-done.9 = f32[3,2,1280]{2,1,0:T(2,128)S(1)} collective-permute-done((f32[3,2,1280]{2,1,0:T(2,128)S(1)}, f32[3,2,1280]{2,1,0:T(2,128)S(1)}, u32[]{:S(2)}, u32[]{:S(2)}) %collective-permute-start.9) | collective-permute-done | bytes 30752 | tf_op jit(solution)/shard_map/ppermute | solution.py:50
  46.2 1.6 %collective-permute-done.10 = f32[3,2,1280]{2,1,0:T(2,128)S(1)} collective-permute-done((f32[3,2,1280]{2,1,0:T(2,128)S(1)}, f32[3,2,1280]{2,1,0:T(2,128)S(1)}, u32[]{:S(2)}, u32[]{:S(2)}) %collective-permute-start.10) | collective-permute-done | bytes 30752 | tf_op jit(solution)/shard_map/ppermute | solution.py:50
  48.0 0.2 reshape.159
  48.1 0.6 fusion.14
  48.8 0.4 multiply_add_fusion
  49.1 0.4 stack.111
  49.6 0.7 broadcast_multiply_fusion
  50.3 0.1 reshape.160
  50.4 0.1 fusion.52
  50.5 0.1 fusion.12
  50.7 0.1 reshape.161
  50.8 0.1 reshape.162
  50.9 1.3 %collective-permute-start.18 = (f32[3,2,1,80]{3,2,1,0:T(1,128)S(1)}, f32[3,2,1,80]{3,2,1,0:T(1,128)S(1)}, u32[]{:S(2)}, u32[]{:S(2)}) collective-permute-start(f32[3,2,1,80]{3,2,1,0:T(1,128)S(1)} %get-tuple-element.79), channel_id=1, source_target_pairs={{0,1},{1,2},{2,3},{4,5},{5,6},{6,7},{8,9},{9,10},{10,11},{12,13},{... | collective-permute-start | bytes 5768 | tf_op jit(solution)/shard_map/ppermute | solution.py:16
  52.1 1.3 %collective-permute-start.19 = (f32[3,2,1,80]{3,2,1,0:T(1,128)S(1)}, f32[3,2,1,80]{3,2,1,0:T(1,128)S(1)}, u32[]{:S(2)}, u32[]{:S(2)}) collective-permute-start(f32[3,2,1,80]{3,2,1,0:T(1,128)S(1)} %get-tuple-element.80), channel_id=1, source_target_pairs={{1,0},{2,1},{3,2},{5,4},{6,5},{7,6},{9,8},{10,9},{11,10},{13,12},{... | collective-permute-start | bytes 5768 | tf_op jit(solution)/shard_map/ppermute | solution.py:17
  53.5 0.1 multiply_reduce_fusion
  53.6 5.0 %collective-permute-done.19 = f32[3,2,1,80]{3,2,1,0:T(1,128)S(1)} collective-permute-done((f32[3,2,1,80]{3,2,1,0:T(1,128)S(1)}, f32[3,2,1,80]{3,2,1,0:T(1,128)S(1)}, u32[]{:S(2)}, u32[]{:S(2)}) %collective-permute-start.19) | collective-permute-done | bytes 1952 | tf_op jit(solution)/shard_map/ppermute | solution.py:17
  58.6 0.1 fusion.2
  58.7 0.1 reshape.163
  58.8 0.1 reshape.164
  59.0 0.1 reshape.165
  59.1 0.1 reduce_sum.38
  59.2 0.1 broadcast_in_dim.115
  59.3 0.1 select_reduce_fusion
  59.4 0.4 copy-done.5
  59.8 3.6 %collective-permute-done.20 = f32[4,16]{1,0:T(4,128)S(1)} collective-permute-done((f32[4,16]{1,0:T(4,128)S(1)}, f32[4,16]{1,0:T(4,128)S(1)}, u32[]{:S(2)}, u32[]{:S(2)}) %collective-permute-start.20) | collective-permute-done | bytes 288 | tf_op jit(solution)/shard_map/ppermute | solution.py:105
  63.4 3.6 %collective-permute-done.21 = f32[4,16]{1,0:T(4,128)S(1)} collective-permute-done((f32[4,16]{1,0:T(4,128)S(1)}, f32[4,16]{1,0:T(4,128)S(1)}, u32[]{:S(2)}, u32[]{:S(2)}) %collective-permute-start.21) | collective-permute-done | bytes 288 | tf_op jit(solution)/shard_map/ppermute | solution.py:105
  67.0 1.9 %collective-permute-start.22 = (f32[4,16]{1,0:T(4,128)S(1)}, f32[4,16]{1,0:T(4,128)S(1)}, u32[]{:S(2)}, u32[]{:S(2)}) collective-permute-start(f32[4,16]{1,0:T(4,128)S(1)} %add.614), channel_id=1, source_target_pairs={{0,16},{4,20},{8,24},{12,28},{16,0},{20,4},{24,8},{28,12},{1,17},{... | collective-permute-start | bytes 776 | tf_op jit(solution)/shard_map/ppermute | solution.py:105
  68.9 2.6 %collective-permute-done.22 = f32[4,16]{1,0:T(4,128)S(1)} collective-permute-done((f32[4,16]{1,0:T(4,128)S(1)}, f32[4,16]{1,0:T(4,128)S(1)}, u32[]{:S(2)}, u32[]{:S(2)}) %collective-permute-start.22) | collective-permute-done | bytes 288 | tf_op jit(solution)/shard_map/ppermute | solution.py:105
  71.5 1.2 %collective-permute-done.23 = f32[4,16]{1,0:T(4,128)S(1)} collective-permute-done((f32[4,16]{1,0:T(4,128)S(1)}, f32[4,16]{1,0:T(4,128)S(1)}, u32[]{:S(2)}, u32[]{:S(2)}) %collective-permute-start.23) | collective-permute-done | bytes 288 | tf_op jit(solution)/shard_map/ppermute | solution.py:105
  72.6 2.3 %collective-permute-start.24 = (f32[4,16]{1,0:T(4,128)S(1)}, f32[4,16]{1,0:T(4,128)S(1)}, u32[]{:S(2)}, u32[]{:S(2)}) collective-permute-start(f32[4,16]{1,0:T(4,128)S(1)} %add.616), channel_id=1, source_target_pairs={{0,2},{1,3},{2,0},{3,1},{4,6},{5,7},{6,4},{7,5},{8,10},{9,11},{10,... | collective-permute-start | bytes 776 | tf_op jit(solution)/shard_map/ppermute | solution.py:105
  74.9 1.6 %collective-permute-done.24 = f32[4,16]{1,0:T(4,128)S(1)} collective-permute-done((f32[4,16]{1,0:T(4,128)S(1)}, f32[4,16]{1,0:T(4,128)S(1)}, u32[]{:S(2)}, u32[]{:S(2)}) %collective-permute-start.24) | collective-permute-done | bytes 288 | tf_op jit(solution)/shard_map/ppermute | solution.py:105
  76.5 0.6 add.617
  (106 shorter events, 1.6 us)
Async XLA Ops:
  2.3 0.7 copy-start.2
  3.1 6.1 %copy-start.4 = (f32[4,2,1280]{2,1,0:T(2,128)S(1)}, f32[4,2,1280]{2,1,0:T(2,128)}, u32[]{:S(2)}) copy-start(f32[4,2,1280]{2,1,0:T(2,128)} %param.7) | copy-start | bytes 122884
  3.1 22.6 %collective-permute-start.11 = (f32[4,2,1280]{2,1,0:T(2,128)S(1)}, f32[4,2,1280]{2,1,0:T(2,128)S(1)}, u32[]{:S(2)}, u32[]{:S(2)}) collective-permute-start(f32[4,2,1280]{2,1,0:T(2,128)S(1)} %pad_maximum_fusion.8), channel_id=1, source_target_pairs={{4,0},{8,4},{12,8},{16,12},{20,16},{24,20},{28,24},{0,28},{5,1},{9... | collective-permute-start | bytes 122888 | tf_op jit(solution)/shard_map/ppermute | solution.py:50
  9.3 11.9 %collective-permute-start = (f32[3,1,16,80]{3,2,0,1:T(8,128)S(1)}, f32[3,1,16,80]{3,2,0,1:T(8,128)S(1)}, u32[]{:S(2)}, u32[]{:S(2)}) collective-permute-start(f32[3,1,16,80]{3,2,0,1:T(8,128)S(1)} %get-tuple-element.83), channel_id=1, source_target_pairs={{0,4},{4,8},{8,12},{12,16},{16,20},{20,24},{24,28},{1,5},{5,9},{9,... | collective-permute-start | bytes 46088 | tf_op jit(solution)/shard_map/ppermute | solution.py:16
  10.6 12.4 %collective-permute-start.1 = (f32[3,1,16,80]{3,2,0,1:T(8,128)S(1)}, f32[3,1,16,80]{3,2,0,1:T(8,128)S(1)}, u32[]{:S(2)}, u32[]{:S(2)}) collective-permute-start(f32[3,1,16,80]{3,2,0,1:T(8,128)S(1)} %get-tuple-element.84), channel_id=1, source_target_pairs={{4,0},{8,4},{12,8},{16,12},{20,16},{24,20},{28,24},{5,1},{9,5},{13... | collective-permute-start | bytes 46088 | tf_op jit(solution)/shard_map/ppermute | solution.py:17
  11.9 4.4 %collective-permute-start.2 = (f32[3,2,1,80]{3,2,1,0:T(1,128)S(1)}, f32[3,2,1,80]{3,2,1,0:T(1,128)S(1)}, u32[]{:S(2)}, u32[]{:S(2)}) collective-permute-start(f32[3,2,1,80]{3,2,1,0:T(1,128)S(1)} %get-tuple-element.87), channel_id=1, source_target_pairs={{0,1},{1,2},{2,3},{4,5},{5,6},{6,7},{8,9},{9,10},{10,11},{12,13},{... | collective-permute-start | bytes 5768 | tf_op jit(solution)/shard_map/ppermute | solution.py:16
  13.4 7.4 %collective-permute-start.3 = (f32[3,2,1,80]{3,2,1,0:T(1,128)S(1)}, f32[3,2,1,80]{3,2,1,0:T(1,128)S(1)}, u32[]{:S(2)}, u32[]{:S(2)}) collective-permute-start(f32[3,2,1,80]{3,2,1,0:T(1,128)S(1)} %get-tuple-element.88), channel_id=1, source_target_pairs={{1,0},{2,1},{3,2},{5,4},{6,5},{7,6},{9,8},{10,9},{11,10},{13,12},{... | collective-permute-start | bytes 5768 | tf_op jit(solution)/shard_map/ppermute | solution.py:17
  14.7 0.7 copy-start.6
  14.7 1.4 %copy-start.1 = (f32[16,2,1280]{2,1,0:T(2,128)S(1)}, f32[16,2,1280]{2,1,0:T(2,128)}, u32[]{:S(2)}) copy-start(f32[16,2,1280]{2,1,0:T(2,128)} %param.10) | copy-start | bytes 491524
  15.4 0.7 copy-start.7
  16.3 12.0 %collective-permute-start.12 = (f32[4,2,1280]{2,1,0:T(2,128)S(1)}, f32[4,2,1280]{2,1,0:T(2,128)S(1)}, u32[]{:S(2)}, u32[]{:S(2)}) collective-permute-start(f32[4,2,1280]{2,1,0:T(2,128)S(1)} %pad_maximum_fusion.8), channel_id=1, source_target_pairs={{8,0},{12,4},{16,8},{20,12},{24,16},{28,20},{0,24},{4,28},{9,1},{1... | collective-permute-start | bytes 122888 | tf_op jit(solution)/shard_map/ppermute | solution.py:50
  20.8 7.6 %collective-permute-start.13 = (f32[4,2,1280]{2,1,0:T(2,128)S(1)}, f32[4,2,1280]{2,1,0:T(2,128)S(1)}, u32[]{:S(2)}, u32[]{:S(2)}) collective-permute-start(f32[4,2,1280]{2,1,0:T(2,128)S(1)} %pad_maximum_fusion.8), channel_id=1, source_target_pairs={{12,0},{16,4},{20,8},{24,12},{28,16},{0,20},{4,24},{8,28},{13,1},{... | collective-permute-start | bytes 122888 | tf_op jit(solution)/shard_map/ppermute | solution.py:50
  21.2 11.9 %collective-permute-start.14 = (f32[4,2,1280]{2,1,0:T(2,128)S(1)}, f32[4,2,1280]{2,1,0:T(2,128)S(1)}, u32[]{:S(2)}, u32[]{:S(2)}) collective-permute-start(f32[4,2,1280]{2,1,0:T(2,128)S(1)} %pad_maximum_fusion.8), channel_id=1, source_target_pairs={{16,0},{20,4},{24,8},{28,12},{0,16},{4,20},{8,24},{12,28},{17,1},{... | collective-permute-start | bytes 122888 | tf_op jit(solution)/shard_map/ppermute | solution.py:50
  23.1 10.2 %collective-permute-start.15 = (f32[4,2,1280]{2,1,0:T(2,128)S(1)}, f32[4,2,1280]{2,1,0:T(2,128)S(1)}, u32[]{:S(2)}, u32[]{:S(2)}) collective-permute-start(f32[4,2,1280]{2,1,0:T(2,128)S(1)} %pad_maximum_fusion.8), channel_id=1, source_target_pairs={{20,0},{24,4},{28,8},{0,12},{4,16},{8,20},{12,24},{16,28},{21,1},{... | collective-permute-start | bytes 122888 | tf_op jit(solution)/shard_map/ppermute | solution.py:50
  24.9 0.8 %copy-start.3 = (f32[4,2,1280]{2,1,0:T(2,128)S(1)}, f32[4,2,1280]{2,1,0:T(2,128)}, u32[]{:S(2)}) copy-start(f32[4,2,1280]{2,1,0:T(2,128)} %param.8) | copy-start | bytes 122884
  25.7 7.6 %collective-permute-start.16 = (f32[4,2,1280]{2,1,0:T(2,128)S(1)}, f32[4,2,1280]{2,1,0:T(2,128)S(1)}, u32[]{:S(2)}, u32[]{:S(2)}) collective-permute-start(f32[4,2,1280]{2,1,0:T(2,128)S(1)} %pad_maximum_fusion.8), channel_id=1, source_target_pairs={{24,0},{28,4},{0,8},{4,12},{8,16},{12,20},{16,24},{20,28},{25,1},{... | collective-permute-start | bytes 122888 | tf_op jit(solution)/shard_map/ppermute | solution.py:50
  28.3 8.0 %collective-permute-start.17 = (f32[4,2,1280]{2,1,0:T(2,128)S(1)}, f32[4,2,1280]{2,1,0:T(2,128)S(1)}, u32[]{:S(2)}, u32[]{:S(2)}) collective-permute-start(f32[4,2,1280]{2,1,0:T(2,128)S(1)} %pad_maximum_fusion.8), channel_id=1, source_target_pairs={{28,0},{0,4},{4,8},{8,12},{12,16},{16,20},{20,24},{24,28},{29,1},{... | collective-permute-start | bytes 122888 | tf_op jit(solution)/shard_map/ppermute | solution.py:50
  28.4 10.6 %collective-permute-start.4 = (f32[3,2,1280]{2,1,0:T(2,128)S(1)}, f32[3,2,1280]{2,1,0:T(2,128)S(1)}, u32[]{:S(2)}, u32[]{:S(2)}) collective-permute-start(f32[3,2,1280]{2,1,0:T(2,128)S(1)} %slice.450), channel_id=1, source_target_pairs={{4,0},{8,4},{12,8},{16,12},{20,16},{24,20},{28,24},{0,28},{5,1},{9... | collective-permute-start | bytes 92168 | tf_op jit(solution)/shard_map/ppermute | solution.py:50
  33.2 8.0 %collective-permute-start.5 = (f32[3,2,1280]{2,1,0:T(2,128)S(1)}, f32[3,2,1280]{2,1,0:T(2,128)S(1)}, u32[]{:S(2)}, u32[]{:S(2)}) collective-permute-start(f32[3,2,1280]{2,1,0:T(2,128)S(1)} %slice.450), channel_id=1, source_target_pairs={{8,0},{12,4},{16,8},{20,12},{24,16},{28,20},{0,24},{4,28},{9,1},{1... | collective-permute-start | bytes 92168 | tf_op jit(solution)/shard_map/ppermute | solution.py:50
  33.3 9.4 %collective-permute-start.6 = (f32[3,2,1280]{2,1,0:T(2,128)S(1)}, f32[3,2,1280]{2,1,0:T(2,128)S(1)}, u32[]{:S(2)}, u32[]{:S(2)}) collective-permute-start(f32[3,2,1280]{2,1,0:T(2,128)S(1)} %slice.450), channel_id=1, source_target_pairs={{12,0},{16,4},{20,8},{24,12},{28,16},{0,20},{4,24},{8,28},{13,1},{... | collective-permute-start | bytes 92168 | tf_op jit(solution)/shard_map/ppermute | solution.py:50
  33.4 9.3 %collective-permute-start.7 = (f32[3,2,1280]{2,1,0:T(2,128)S(1)}, f32[3,2,1280]{2,1,0:T(2,128)S(1)}, u32[]{:S(2)}, u32[]{:S(2)}) collective-permute-start(f32[3,2,1280]{2,1,0:T(2,128)S(1)} %slice.450), channel_id=1, source_target_pairs={{16,0},{20,4},{24,8},{28,12},{0,16},{4,20},{8,24},{12,28},{17,1},{... | collective-permute-start | bytes 92168 | tf_op jit(solution)/shard_map/ppermute | solution.py:50
  36.3 6.3 %collective-permute-start.8 = (f32[3,2,1280]{2,1,0:T(2,128)S(1)}, f32[3,2,1280]{2,1,0:T(2,128)S(1)}, u32[]{:S(2)}, u32[]{:S(2)}) collective-permute-start(f32[3,2,1280]{2,1,0:T(2,128)S(1)} %slice.450), channel_id=1, source_target_pairs={{20,0},{24,4},{28,8},{0,12},{4,16},{8,20},{12,24},{16,28},{21,1},{... | collective-permute-start | bytes 92168 | tf_op jit(solution)/shard_map/ppermute | solution.py:50
  36.6 0.7 copy-start
  37.4 0.9 %slice-start = ((f32[4,8,2,1280]{3,2,0,1:T(2,128)}), f32[1,8,2,1280]{3,2,0,1:T(2,128)S(1)}, s32[]{:S(2)}) async-start(f32[4,8,2,1280]{3,2,0,1:T(2,128)} %copy-done), calls=%async_computation | async-start | bytes 163840 | tf_op jit(solution)/shard_map/slice | solution.py:139
  39.0 7.2 %collective-permute-start.9 = (f32[3,2,1280]{2,1,0:T(2,128)S(1)}, f32[3,2,1280]{2,1,0:T(2,128)S(1)}, u32[]{:S(2)}, u32[]{:S(2)}) collective-permute-start(f32[3,2,1280]{2,1,0:T(2,128)S(1)} %slice.450), channel_id=1, source_target_pairs={{24,0},{28,4},{0,8},{4,12},{8,16},{12,20},{16,24},{20,28},{25,1},{... | collective-permute-start | bytes 92168 | tf_op jit(solution)/shard_map/ppermute | solution.py:50
  41.1 6.6 %collective-permute-start.10 = (f32[3,2,1280]{2,1,0:T(2,128)S(1)}, f32[3,2,1280]{2,1,0:T(2,128)S(1)}, u32[]{:S(2)}, u32[]{:S(2)}) collective-permute-start(f32[3,2,1280]{2,1,0:T(2,128)S(1)} %slice.450), channel_id=1, source_target_pairs={{28,0},{0,4},{4,8},{8,12},{12,16},{16,20},{20,24},{24,28},{29,1},{... | collective-permute-start | bytes 92168 | tf_op jit(solution)/shard_map/ppermute | solution.py:50
  50.9 2.7 %collective-permute-start.18 = (f32[3,2,1,80]{3,2,1,0:T(1,128)S(1)}, f32[3,2,1,80]{3,2,1,0:T(1,128)S(1)}, u32[]{:S(2)}, u32[]{:S(2)}) collective-permute-start(f32[3,2,1,80]{3,2,1,0:T(1,128)S(1)} %get-tuple-element.79), channel_id=1, source_target_pairs={{0,1},{1,2},{2,3},{4,5},{5,6},{6,7},{8,9},{9,10},{10,11},{12,13},{... | collective-permute-start | bytes 5768 | tf_op jit(solution)/shard_map/ppermute | solution.py:16
  52.1 6.5 %collective-permute-start.19 = (f32[3,2,1,80]{3,2,1,0:T(1,128)S(1)}, f32[3,2,1,80]{3,2,1,0:T(1,128)S(1)}, u32[]{:S(2)}, u32[]{:S(2)}) collective-permute-start(f32[3,2,1,80]{3,2,1,0:T(1,128)S(1)} %get-tuple-element.80), channel_id=1, source_target_pairs={{1,0},{2,1},{3,2},{5,4},{6,5},{7,6},{9,8},{10,9},{11,10},{13,12},{... | collective-permute-start | bytes 5768 | tf_op jit(solution)/shard_map/ppermute | solution.py:17
  59.2 0.6 copy-start.5
  59.8 3.6 %collective-permute-start.20 = (f32[4,16]{1,0:T(4,128)S(1)}, f32[4,16]{1,0:T(4,128)S(1)}, u32[]{:S(2)}, u32[]{:S(2)}) collective-permute-start(f32[4,16]{1,0:T(4,128)S(1)} %select_reduce_fusion), channel_id=1, source_target_pairs={{0,4},{4,0},{8,12},{12,8},{16,20},{20,16},{24,28},{28,24},{1,5},{5... | collective-permute-start | bytes 776 | tf_op jit(solution)/shard_map/ppermute | solution.py:105
  63.4 3.6 %collective-permute-start.21 = (f32[4,16]{1,0:T(4,128)S(1)}, f32[4,16]{1,0:T(4,128)S(1)}, u32[]{:S(2)}, u32[]{:S(2)}) collective-permute-start(f32[4,16]{1,0:T(4,128)S(1)} %add.613), channel_id=1, source_target_pairs={{0,8},{4,12},{8,0},{12,4},{16,24},{20,28},{24,16},{28,20},{1,9},{5... | collective-permute-start | bytes 776 | tf_op jit(solution)/shard_map/ppermute | solution.py:105
  67.0 4.5 %collective-permute-start.22 = (f32[4,16]{1,0:T(4,128)S(1)}, f32[4,16]{1,0:T(4,128)S(1)}, u32[]{:S(2)}, u32[]{:S(2)}) collective-permute-start(f32[4,16]{1,0:T(4,128)S(1)} %add.614), channel_id=1, source_target_pairs={{0,16},{4,20},{8,24},{12,28},{16,0},{20,4},{24,8},{28,12},{1,17},{... | collective-permute-start | bytes 776 | tf_op jit(solution)/shard_map/ppermute | solution.py:105
  71.5 1.2 %collective-permute-start.23 = (f32[4,16]{1,0:T(4,128)S(1)}, f32[4,16]{1,0:T(4,128)S(1)}, u32[]{:S(2)}, u32[]{:S(2)}) collective-permute-start(f32[4,16]{1,0:T(4,128)S(1)} %add.615), channel_id=1, source_target_pairs={{0,1},{1,0},{2,3},{3,2},{4,5},{5,4},{6,7},{7,6},{8,9},{9,8},{10,11... | collective-permute-start | bytes 776 | tf_op jit(solution)/shard_map/ppermute | solution.py:105
  72.6 3.8 %collective-permute-start.24 = (f32[4,16]{1,0:T(4,128)S(1)}, f32[4,16]{1,0:T(4,128)S(1)}, u32[]{:S(2)}, u32[]{:S(2)}) collective-permute-start(f32[4,16]{1,0:T(4,128)S(1)} %add.616), channel_id=1, source_target_pairs={{0,2},{1,3},{2,0},{3,1},{4,6},{5,7},{6,4},{7,5},{8,10},{9,11},{10,... | collective-permute-start | bytes 776 | tf_op jit(solution)/shard_map/ppermute | solution.py:105

commit v3 on v1

--- a/solution.py
+++ b/solution.py
@@ -28,9 +28,12 @@
 
 def neighbour_terms(grid_view, x_low, x_high, y_low, y_high, viscosity, frozen):
     shape = grid_view.shape
-    x_pad = jnp.concatenate([x_low, grid_view, x_high], axis=1)
     y_pad = jnp.concatenate([y_low, grid_view, y_high], axis=2)
-    along_line = 2.0 * grid_view - x_pad[:, :-2] - x_pad[:, 2:]
+    if x_low is None:
+        along_line = 2.0 * grid_view
+    else:
+        x_pad = jnp.concatenate([x_low, grid_view, x_high], axis=1)
+        along_line = 2.0 * grid_view - x_pad[:, :-2] - x_pad[:, 2:]
     across_line = y_pad[:, :, :-2] + y_pad[:, :, 2:] + vertical_pair(grid_view, frozen)
     flat = (3, shape[1], shape[2] * shape[3])
     return viscosity * along_line.reshape(flat) - coupling * viscosity * across_line.reshape(flat)
@@ -123,24 +126,27 @@
 
     masked = solution * active[None]
     masked_grid = masked[:3].reshape(grid)
-    x_low, x_high = neighbour_shift(masked_grid, "gx", 1, 1)
     y_low, y_high = neighbour_shift(masked_grid, "gy", 2, 1)
     in_cell = in_cell_terms(masked, matrix)
-    moving = in_cell[:3] + neighbour_terms(masked_grid, x_low, x_high, y_low, y_high, viscosity, frozen)
+    moving = in_cell[:3] + neighbour_terms(masked_grid, None, None, y_low, y_high, viscosity, frozen)
     residual = active[None] * (forcing - jnp.concatenate([moving, in_cell[3:]], axis=0))
 
     diagonal = jnp.stack([matrix[0, 0], matrix[1, 1], matrix[2, 2]])
     line_lead = jnp.where(active[None] > 0.0, diagonal + 2.0 * viscosity[None], 1.0)
     line_off = (viscosity * active)[None]
-    packed = jnp.concatenate([line_lead, line_off, residual[:3]], axis=0)
+    packed = jnp.concatenate([line_lead, line_off, residual[:3], masked[:3]], axis=0)
     whole = gather_rows(packed, "gx")
     all_rows = whole.shape[1]
+    whole_off = whole[3:4]
+    padded_masked = jnp.pad(whole[7:10], ((0, 0), (1, 1), (0, 0)))
+    whole_rhs = whole[4:7] + whole_off * (padded_masked[:, :-2] + padded_masked[:, 2:])
     solver = line_solve if all_rows <= 32 else line_solve_scan
-    whole_corr = solver(whole[0:3], jnp.broadcast_to(whole[3:4], (3,) + whole.shape[1:]), whole[4:7])
+    whole_corr = solver(whole[0:3], jnp.broadcast_to(whole_off, whole_rhs.shape), whole_rhs)
 
     first = lax.axis_index("gx") * row_count
     padded_corr = jnp.pad(whole_corr, ((0, 0), (1, 1), (0, 0)))
     near_corr = lax.dynamic_slice_in_dim(padded_corr, first, row_count + 2, axis=1)
+    near_masked = lax.dynamic_slice_in_dim(padded_masked, first, row_count + 2, axis=1)
     correction = near_corr[:, 1:-1]
 
     pressure_in = residual[3] - (
@@ -153,8 +159,8 @@
     smoothed_masked = smoothed * active[None]
     sm_grid = smoothed_masked[:3].reshape(grid)
     edge = (3, 1, y_cells, LAYERS)
-    x_low2 = x_low + near_corr[:, :1].reshape(edge)
-    x_high2 = x_high + near_corr[:, -1:].reshape(edge)
+    x_low2 = (near_masked[:, :1] + near_corr[:, :1]).reshape(edge)
+    x_high2 = (near_masked[:, -1:] + near_corr[:, -1:]).reshape(edge)
     y_low2, y_high2 = neighbour_shift(sm_grid, "gy", 2, 1)
     in_cell2 = in_cell_terms(smoothed_masked, matrix)
     moving2 = in_cell2[:3] + neighbour_terms(sm_grid, x_low2, x_high2, y_low2, y_high2, viscosity, frozen)

time: 68 us -> 66.6 us (0.979)
  starting transfers between devices: 29.6 us -> 25.9 us
  waiting for transfers between devices: 24.6 us -> 26.7 us
    ppermute x7, waiting for transfers between devices: 8.35 us -> 13.8 us  [gather_rows(): pieces.append(lax.ppermute(block, axis, pairs))]
    ppermute x3 -> x2, starting transfers between devices: 9.4 us -> 5.66 us  [neighbour_shift(): lax.ppermute(lax.slice_in_dim(block, block.shape[dim] - width, None, axis...]
    ppermute x3 -> x2, waiting for transfers between devices: 3.43 us -> 0.01 us  [neighbour_shift(): lax.ppermute(lax.slice_in_dim(block, 0, width, axis=dim), axis, backward)]
    ppermute x5, starting transfers between devices: 3.84 us -> 5.73 us  [tree_sum(): lax.ppermute(value, axis, [(i, i ^ step) for i in range(count)])]
    ppermute x3 -> x2, starting transfers between devices: 3.88 us -> 2.58 us  [neighbour_shift(): lax.ppermute(lax.slice_in_dim(block, 0, width, axis=dim), axis, backward)]
    broadcast_in_dim x0 -> x1, other arithmetic: none -> 0.72 us  [local(): line_off = (viscosity * active)[None]]
    mul x1 -> x0, other arithmetic: 0.72 us -> none  [local(): 2.0 * viscosity[None]]
  transfers between devices with their start and end apart: 18 -> 16, of which waited for: 8 -> 8; matrix products, arithmetic and copies ran while one was open for 6% -> 7% of each run, Pallas kernels for 0% -> 0%
where the time goes in v3:
time: 66.6 us; the launch traced here: 66.1 us
  waiting for transfers between devices  26.7 us (40%)
  starting transfers between devices  25.9 us (39%)
  other arithmetic  7.33 us (11%)
  local copies, waits for them, and re-layouts  5.03 us (8%)
  between operations  1.17 us (2%)
    ppermute x7, waiting for transfers between devices, gather_rows(): pieces.append(lax.ppermute(block, axis, pairs))  13.8 us
    ppermute x5, waiting for transfers between devices, tree_sum(): lax.ppermute(value, axis, [(i, i ^ step) for i in range(count)])  12.5 us
    ppermute x7, starting transfers between devices, gather_rows(): pieces.append(lax.ppermute(block, axis, pairs))  11.9 us
    ppermute x5, starting transfers between devices, tree_sum(): lax.ppermute(value, axis, [(i, i ^ step) for i in range(count)])  5.73 us
    ppermute x2, starting transfers between devices, neighbour_shift(): lax.ppermute(lax.slice_in_dim(block, block.shape[dim] - width, None, axis...  5.66 us
    ppermute x2, starting transfers between devices, neighbour_shift(): lax.ppermute(lax.slice_in_dim(block, 0, width, axis=dim), axis, backward)  2.58 us
  transfers between devices with their start and end apart: 16, of which 8 were waited for; matrix products, arithmetic and copies ran while one was open for 7% of the time, Pallas kernels for 0%

profile of v3, /device:TPU:0, one launch (start us, length us, event | category | flops | bytes accessed | tf_op | source)
XLA Modules:
  0.0 66.1 jit_solution(10263700732359799369)
XLA Ops:
  0.6 0.8 %lt.38 = s32[2,16,80]{2,1,0:T(8,128)S(1)} broadcast(s32[2,16]{1,0:T(2,128)} %param.11), dimensions={0,1} | broadcast | bytes 10368 | tf_op jit(solution)/shard_map/lt | solution.py:119
  1.4 0.1 lt.39
  1.5 0.1 lt.36
  1.6 0.8 %broadcast_multiply_fusion.1 = f32[1,8,1280]{2,1,0:T(8,128)S(1)} fusion(f32[1,8,1280]{2,1,0:T(8,128)} %bitcast.108, f32[8,1280]{1,0:T(8,128)S(1)} %bitcast.107), kind=kLoop, calls=%fused_computation.60 | loop fusion | flops 10240 | bytes 122880 | tf_op jit(solution)/shard_map/mul | solution.py:127
  2.4 0.1 reshape.153
  2.5 2.4 %collective-permute-start = (f32[3,2,1,80]{3,2,1,0:T(1,128)S(1)}, f32[3,2,1,80]{3,2,1,0:T(1,128)S(1)}, u32[]{:S(2)}, u32[]{:S(2)}) collective-permute-start(f32[3,2,1,80]{3,2,1,0:T(1,128)S(1)} %get-tuple-element.86), channel_id=1, source_target_pairs={{0,1},{1,2},{2,3},{4,5},{5,6},{6,7},{8,9},{9,10},{10,11},{12,13},{... | collective-permute-start | bytes 5768 | tf_op jit(solution)/shard_map/ppermute | solution.py:16
  5.0 1.3 %collective-permute-start.1 = (f32[3,2,1,80]{3,2,1,0:T(1,128)S(1)}, f32[3,2,1,80]{3,2,1,0:T(1,128)S(1)}, u32[]{:S(2)}, u32[]{:S(2)}) collective-permute-start(f32[3,2,1,80]{3,2,1,0:T(1,128)S(1)} %get-tuple-element.87), channel_id=1, source_target_pairs={{1,0},{2,1},{3,2},{5,4},{6,5},{7,6},{9,8},{10,9},{11,10},{13,12},{... | collective-permute-start | bytes 5768 | tf_op jit(solution)/shard_map/ppermute | solution.py:17
  6.3 0.1 fusion.58
  6.3 0.7 %convert_subtract_fusion = f32[2,16]{1,0:T(2,128)S(1)} fusion(s32[2,16]{1,0:T(2,128)} %param.12), kind=kLoop, calls=%fused_computation.183 | loop fusion | flops 64 | bytes 256 | tf_op jit(solution)/shard_map/sub | solution.py:23
  7.0 0.1 slice_multiply_fusion.1
  7.1 0.7 %select_bitcast_fusion = (f32[1,2,1280]{2,1,0:T(2,128)S(1)}, f32[2,1280]{1,0:T(2,128)S(1)}, f32[2,1280]{1,0:T(2,128)S(1)}) fusion(pred[2,1280]{1,0:T(4,128)(4,1)S(1)} %get-tuple-element.71, f32[2,1280]{1,0:T(2,128)} %param.9), kind=kLoop, calls=%fused_computation.144 | loop fusion | flops 7680 | bytes 43520 | tf_op jit(solution)/shard_map/broadcast_in_dim | solution.py:136
  7.8 0.7 %slice_bitcast_fusion.6 = (f32[1,2,1280]{2,1,0:T(2,128)S(1)}, f32[1,2,1280]{2,1,0:T(2,128)S(1)}, f32[1,2,1280]{2,1,0:T(2,128)S(1)}) fusion(f32[4,4,2,1280]{3,2,1,0:T(2,128)} %bitcast.102), kind=kLoop, calls=%fused_computation.143 | loop fusion | bytes 61440 | tf_op jit(solution)/shard_map/stack;squeeze | solution.py:134
  8.6 0.8 %eq.19 = s32[32]{0:T(128)S(1)} reshape(s32[2,16]{1,0:T(2,128)} %param.13) | data formatting | bytes 256 | tf_op jit(solution)/shard_map/eq | solution.py:171
  9.3 1.0 %multiply_reduce_fusion.1 = f32[4,2,1280]{2,1,0:T(2,128)S(1)} fusion(f32[4,2,1280]{2,1,0:T(2,128)S(1)} %bitcast.105, f32[16,2,1280]{2,1,0:T(2,128)} %param.10), kind=kLoop, calls=%fused_computation.15 | loop fusion | flops 71680 | bytes 245760 | tf_op jit(solution)/shard_map/reduce_sum | solution.py:43
  10.4 0.1 fusion.8
  10.5 0.1 reshape.154
  10.6 0.1 fusion.11
  10.8 5.4 %collective-permute-start.2 = (f32[10,2,1280]{2,1,0:T(2,128)S(1)}, f32[10,2,1280]{2,1,0:T(2,128)S(1)}, u32[]{:S(2)}, u32[]{:S(2)}) collective-permute-start(f32[10,2,1280]{2,1,0:T(2,128)S(1)} %pad_maximum_fusion), channel_id=1, source_target_pairs={{4,0},{8,4},{12,8},{16,12},{20,16},{24,20},{28,24},{0,28},{5,1},{9... | collective-permute-start | bytes 307208 | tf_op jit(solution)/shard_map/ppermute | solution.py:53
  16.2 0.5 collective-permute-start.3
  16.7 3.0 %collective-permute-start.5 = (f32[10,2,1280]{2,1,0:T(2,128)S(1)}, f32[10,2,1280]{2,1,0:T(2,128)S(1)}, u32[]{:S(2)}, u32[]{:S(2)}) collective-permute-start(f32[10,2,1280]{2,1,0:T(2,128)S(1)} %pad_maximum_fusion), channel_id=1, source_target_pairs={{16,0},{20,4},{24,8},{28,12},{0,16},{4,20},{8,24},{12,28},{17,1},{... | collective-permute-start | bytes 307208 | tf_op jit(solution)/shard_map/ppermute | solution.py:53
  19.7 1.8 %collective-permute-start.7 = (f32[10,2,1280]{2,1,0:T(2,128)S(1)}, f32[10,2,1280]{2,1,0:T(2,128)S(1)}, u32[]{:S(2)}, u32[]{:S(2)}) collective-permute-start(f32[10,2,1280]{2,1,0:T(2,128)S(1)} %pad_maximum_fusion), channel_id=1, source_target_pairs={{24,0},{28,4},{0,8},{4,12},{8,16},{12,20},{16,24},{20,28},{25,1},{... | collective-permute-start | bytes 307208 | tf_op jit(solution)/shard_map/ppermute | solution.py:53
  21.6 1.2 %collective-permute-start.8 = (f32[10,2,1280]{2,1,0:T(2,128)S(1)}, f32[10,2,1280]{2,1,0:T(2,128)S(1)}, u32[]{:S(2)}, u32[]{:S(2)}) collective-permute-start(f32[10,2,1280]{2,1,0:T(2,128)S(1)} %pad_maximum_fusion), channel_id=1, source_target_pairs={{28,0},{0,4},{4,8},{8,12},{12,16},{16,20},{20,24},{24,28},{29,1},{... | collective-permute-start | bytes 307208 | tf_op jit(solution)/shard_map/ppermute | solution.py:53
  22.8 11.5 %collective-permute-done.5 = f32[10,2,1280]{2,1,0:T(2,128)S(1)} collective-permute-done((f32[10,2,1280]{2,1,0:T(2,128)S(1)}, f32[10,2,1280]{2,1,0:T(2,128)S(1)}, u32[]{:S(2)}, u32[]{:S(2)}) %collective-permute-start.5) | collective-permute-done | bytes 102432 | tf_op jit(solution)/shard_map/ppermute | solution.py:53
  34.4 2.3 %collective-permute-done.6 = f32[10,2,1280]{2,1,0:T(2,128)S(1)} collective-permute-done((f32[10,2,1280]{2,1,0:T(2,128)S(1)}, f32[10,2,1280]{2,1,0:T(2,128)S(1)}, u32[]{:S(2)}, u32[]{:S(2)}) %collective-permute-start.6) | collective-permute-done | bytes 102432 | tf_op jit(solution)/shard_map/ppermute | solution.py:53
  36.7 0.1 bitcast_dynamic-update-slice_fusion.15
  37.0 0.1 dynamic-slice_bitcast_fusion
  37.1 0.1 fusion.55
  37.2 0.2 slice.368
  37.4 0.1 mul.968
  37.5 0.2 slice_reduce_fusion
  37.7 0.2 slice.359
  37.9 0.2 slice.362
  38.1 0.1 fusion.2
  38.2 0.4 broadcast_divide_fusion
  38.7 0.6 fusion.15
  39.3 0.4 multiply_add_fusion
  39.6 0.4 stack.32
  40.1 0.1 fusion.40
  40.2 0.7 broadcast_multiply_fusion
  40.8 0.1 reshape.155
  40.9 0.1 fusion.56
  41.0 0.1 slice_multiply_fusion
  41.1 0.1 multiply_reduce_fusion
  41.2 1.3 %collective-permute-start.10 = (f32[3,2,1,80]{3,2,1,0:T(1,128)S(1)}, f32[3,2,1,80]{3,2,1,0:T(1,128)S(1)}, u32[]{:S(2)}, u32[]{:S(2)}) collective-permute-start(f32[3,2,1,80]{3,2,1,0:T(1,128)S(1)} %get-tuple-element.83), channel_id=1, source_target_pairs={{1,0},{2,1},{3,2},{5,4},{6,5},{7,6},{9,8},{10,9},{11,10},{13,12},{... | collective-permute-start | bytes 5768 | tf_op jit(solution)/shard_map/ppermute | solution.py:17
  42.5 3.3 %collective-permute-start.9 = (f32[3,2,1,80]{3,2,1,0:T(1,128)S(1)}, f32[3,2,1,80]{3,2,1,0:T(1,128)S(1)}, u32[]{:S(2)}, u32[]{:S(2)}) collective-permute-start(f32[3,2,1,80]{3,2,1,0:T(1,128)S(1)} %get-tuple-element.82), channel_id=1, source_target_pairs={{0,1},{1,2},{2,3},{4,5},{5,6},{6,7},{8,9},{9,10},{10,11},{12,13},{... | collective-permute-start | bytes 5768 | tf_op jit(solution)/shard_map/ppermute | solution.py:16
  45.7 0.2 fusion.30
  45.9 0.1 reshape.156
  46.0 0.1 reshape.157
  46.1 0.4 collective-permute-done.9
  46.5 0.1 fusion.5
  46.6 0.1 reshape.158
  46.7 0.1 reshape.159
  46.9 0.1 reshape.160
  47.0 0.1 reduce_sum.38
  47.2 0.1 broadcast_in_dim.61
  47.2 0.1 select_reduce_fusion
  47.3 3.6 %collective-permute-done.11 = f32[4,16]{1,0:T(4,128)S(1)} collective-permute-done((f32[4,16]{1,0:T(4,128)S(1)}, f32[4,16]{1,0:T(4,128)S(1)}, u32[]{:S(2)}, u32[]{:S(2)}) %collective-permute-start.11) | collective-permute-done | bytes 288 | tf_op jit(solution)/shard_map/ppermute | solution.py:108
  50.9 3.6 %collective-permute-done.12 = f32[4,16]{1,0:T(4,128)S(1)} collective-permute-done((f32[4,16]{1,0:T(4,128)S(1)}, f32[4,16]{1,0:T(4,128)S(1)}, u32[]{:S(2)}, u32[]{:S(2)}) %collective-permute-start.12) | collective-permute-done | bytes 288 | tf_op jit(solution)/shard_map/ppermute | solution.py:108
  54.5 1.9 %collective-permute-start.13 = (f32[4,16]{1,0:T(4,128)S(1)}, f32[4,16]{1,0:T(4,128)S(1)}, u32[]{:S(2)}, u32[]{:S(2)}) collective-permute-start(f32[4,16]{1,0:T(4,128)S(1)} %add.624), channel_id=1, source_target_pairs={{0,16},{4,20},{8,24},{12,28},{16,0},{20,4},{24,8},{28,12},{1,17},{... | collective-permute-start | bytes 776 | tf_op jit(solution)/shard_map/ppermute | solution.py:108
  56.4 2.6 %collective-permute-done.13 = f32[4,16]{1,0:T(4,128)S(1)} collective-permute-done((f32[4,16]{1,0:T(4,128)S(1)}, f32[4,16]{1,0:T(4,128)S(1)}, u32[]{:S(2)}, u32[]{:S(2)}) %collective-permute-start.13) | collective-permute-done | bytes 288 | tf_op jit(solution)/shard_map/ppermute | solution.py:108
  59.0 1.2 %collective-permute-done.14 = f32[4,16]{1,0:T(4,128)S(1)} collective-permute-done((f32[4,16]{1,0:T(4,128)S(1)}, f32[4,16]{1,0:T(4,128)S(1)}, u32[]{:S(2)}, u32[]{:S(2)}) %collective-permute-start.14) | collective-permute-done | bytes 288 | tf_op jit(solution)/shard_map/ppermute | solution.py:108
  60.2 3.8 %collective-permute-start.15 = (f32[4,16]{1,0:T(4,128)S(1)}, f32[4,16]{1,0:T(4,128)S(1)}, u32[]{:S(2)}, u32[]{:S(2)}) collective-permute-start(f32[4,16]{1,0:T(4,128)S(1)} %add.626), channel_id=1, source_target_pairs={{0,2},{1,3},{2,0},{3,1},{4,6},{5,7},{6,4},{7,5},{8,10},{9,11},{10,... | collective-permute-start | bytes 776 | tf_op jit(solution)/shard_map/ppermute | solution.py:108
  64.0 1.6 %collective-permute-done.15 = f32[4,16]{1,0:T(4,128)S(1)} collective-permute-done((f32[4,16]{1,0:T(4,128)S(1)}, f32[4,16]{1,0:T(4,128)S(1)}, u32[]{:S(2)}, u32[]{:S(2)}) %collective-permute-start.15) | collective-permute-done | bytes 288 | tf_op jit(solution)/shard_map/ppermute | solution.py:108
  65.6 0.6 add.627
  (63 shorter events, 0.7 us)
Async XLA Ops:
  0.6 10.0 %copy-start.1 = (f32[4,2,1280]{2,1,0:T(2,128)S(1)}, f32[4,2,1280]{2,1,0:T(2,128)}, u32[]{:S(2)}) copy-start(f32[4,2,1280]{2,1,0:T(2,128)} %param.8) | copy-start | bytes 122884
  2.5 7.8 %collective-permute-start = (f32[3,2,1,80]{3,2,1,0:T(1,128)S(1)}, f32[3,2,1,80]{3,2,1,0:T(1,128)S(1)}, u32[]{:S(2)}, u32[]{:S(2)}) collective-permute-start(f32[3,2,1,80]{3,2,1,0:T(1,128)S(1)} %get-tuple-element.86), channel_id=1, source_target_pairs={{0,1},{1,2},{2,3},{4,5},{5,6},{6,7},{8,9},{9,10},{10,11},{12,13},{... | collective-permute-start | bytes 5768 | tf_op jit(solution)/shard_map/ppermute | solution.py:16
  5.0 5.4 %collective-permute-start.1 = (f32[3,2,1,80]{3,2,1,0:T(1,128)S(1)}, f32[3,2,1,80]{3,2,1,0:T(1,128)S(1)}, u32[]{:S(2)}, u32[]{:S(2)}) collective-permute-start(f32[3,2,1,80]{3,2,1,0:T(1,128)S(1)} %get-tuple-element.87), channel_id=1, source_target_pairs={{1,0},{2,1},{3,2},{5,4},{6,5},{7,6},{9,8},{10,9},{11,10},{13,12},{... | collective-permute-start | bytes 5768 | tf_op jit(solution)/shard_map/ppermute | solution.py:17
  10.8 9.0 %collective-permute-start.2 = (f32[10,2,1280]{2,1,0:T(2,128)S(1)}, f32[10,2,1280]{2,1,0:T(2,128)S(1)}, u32[]{:S(2)}, u32[]{:S(2)}) collective-permute-start(f32[10,2,1280]{2,1,0:T(2,128)S(1)} %pad_maximum_fusion), channel_id=1, source_target_pairs={{4,0},{8,4},{12,8},{16,12},{20,16},{24,20},{28,24},{0,28},{5,1},{9... | collective-permute-start | bytes 307208 | tf_op jit(solution)/shard_map/ppermute | solution.py:53
  16.2 5.4 %collective-permute-start.3 = (f32[10,2,1280]{2,1,0:T(2,128)S(1)}, f32[10,2,1280]{2,1,0:T(2,128)S(1)}, u32[]{:S(2)}, u32[]{:S(2)}) collective-permute-start(f32[10,2,1280]{2,1,0:T(2,128)S(1)} %pad_maximum_fusion), channel_id=1, source_target_pairs={{8,0},{12,4},{16,8},{20,12},{24,16},{28,20},{0,24},{4,28},{9,1},{1... | collective-permute-start | bytes 307208 | tf_op jit(solution)/shard_map/ppermute | solution.py:53
  16.7 6.1 %collective-permute-start.4 = (f32[10,2,1280]{2,1,0:T(2,128)S(1)}, f32[10,2,1280]{2,1,0:T(2,128)S(1)}, u32[]{:S(2)}, u32[]{:S(2)}) collective-permute-start(f32[10,2,1280]{2,1,0:T(2,128)S(1)} %pad_maximum_fusion), channel_id=1, source_target_pairs={{12,0},{16,4},{20,8},{24,12},{28,16},{0,20},{4,24},{8,28},{13,1},{... | collective-permute-start | bytes 307208 | tf_op jit(solution)/shard_map/ppermute | solution.py:53
  16.7 17.6 %collective-permute-start.5 = (f32[10,2,1280]{2,1,0:T(2,128)S(1)}, f32[10,2,1280]{2,1,0:T(2,128)S(1)}, u32[]{:S(2)}, u32[]{:S(2)}) collective-permute-start(f32[10,2,1280]{2,1,0:T(2,128)S(1)} %pad_maximum_fusion), channel_id=1, source_target_pairs={{16,0},{20,4},{24,8},{28,12},{0,16},{4,20},{8,24},{12,28},{17,1},{... | collective-permute-start | bytes 307208 | tf_op jit(solution)/shard_map/ppermute | solution.py:53
  19.7 16.9 %collective-permute-start.6 = (f32[10,2,1280]{2,1,0:T(2,128)S(1)}, f32[10,2,1280]{2,1,0:T(2,128)S(1)}, u32[]{:S(2)}, u32[]{:S(2)}) collective-permute-start(f32[10,2,1280]{2,1,0:T(2,128)S(1)} %pad_maximum_fusion), channel_id=1, source_target_pairs={{20,0},{24,4},{28,8},{0,12},{4,16},{8,20},{12,24},{16,28},{21,1},{... | collective-permute-start | bytes 307208 | tf_op jit(solution)/shard_map/ppermute | solution.py:53
  19.7 16.9 %collective-permute-start.7 = (f32[10,2,1280]{2,1,0:T(2,128)S(1)}, f32[10,2,1280]{2,1,0:T(2,128)S(1)}, u32[]{:S(2)}, u32[]{:S(2)}) collective-permute-start(f32[10,2,1280]{2,1,0:T(2,128)S(1)} %pad_maximum_fusion), channel_id=1, source_target_pairs={{24,0},{28,4},{0,8},{4,12},{8,16},{12,20},{16,24},{20,28},{25,1},{... | collective-permute-start | bytes 307208 | tf_op jit(solution)/shard_map/ppermute | solution.py:53
  21.6 15.1 %collective-permute-start.8 = (f32[10,2,1280]{2,1,0:T(2,128)S(1)}, f32[10,2,1280]{2,1,0:T(2,128)S(1)}, u32[]{:S(2)}, u32[]{:S(2)}) collective-permute-start(f32[10,2,1280]{2,1,0:T(2,128)S(1)} %pad_maximum_fusion), channel_id=1, source_target_pairs={{28,0},{0,4},{4,8},{8,12},{12,16},{16,20},{20,24},{24,28},{29,1},{... | collective-permute-start | bytes 307208 | tf_op jit(solution)/shard_map/ppermute | solution.py:53
  38.2 1.9 %copy-start = (f32[16,2,1280]{2,1,0:T(2,128)S(1)}, f32[16,2,1280]{2,1,0:T(2,128)}, u32[]{:S(2)}) copy-start(f32[16,2,1280]{2,1,0:T(2,128)} %param.10) | copy-start | bytes 491524
  38.2 1.9 %copy-start.3 = (f32[2,1280]{1,0:T(2,128)S(1)}, f32[2,1280]{1,0:T(2,128)}, u32[]{:S(2)}) copy-start(f32[2,1280]{1,0:T(2,128)} %param.9) | copy-start | bytes 30724
  38.2 1.9 %copy-start.2 = (f32[4,2,1280]{2,1,0:T(2,128)S(1)}, f32[4,2,1280]{2,1,0:T(2,128)}, u32[]{:S(2)}) copy-start(f32[4,2,1280]{2,1,0:T(2,128)} %param.7) | copy-start | bytes 122884
  41.2 4.9 %collective-permute-start.10 = (f32[3,2,1,80]{3,2,1,0:T(1,128)S(1)}, f32[3,2,1,80]{3,2,1,0:T(1,128)S(1)}, u32[]{:S(2)}, u32[]{:S(2)}) collective-permute-start(f32[3,2,1,80]{3,2,1,0:T(1,128)S(1)} %get-tuple-element.83), channel_id=1, source_target_pairs={{1,0},{2,1},{3,2},{5,4},{6,5},{7,6},{9,8},{10,9},{11,10},{13,12},{... | collective-permute-start | bytes 5768 | tf_op jit(solution)/shard_map/ppermute | solution.py:17
  42.5 4.1 %collective-permute-start.9 = (f32[3,2,1,80]{3,2,1,0:T(1,128)S(1)}, f32[3,2,1,80]{3,2,1,0:T(1,128)S(1)}, u32[]{:S(2)}, u32[]{:S(2)}) collective-permute-start(f32[3,2,1,80]{3,2,1,0:T(1,128)S(1)} %get-tuple-element.82), channel_id=1, source_target_pairs={{0,1},{1,2},{2,3},{4,5},{5,6},{6,7},{8,9},{9,10},{10,11},{12,13},{... | collective-permute-start | bytes 5768 | tf_op jit(solution)/shard_map/ppermute | solution.py:16
  47.1 19.0 %copy-start.4 = (f32[4,2,16]{2,1,0:T(2,128)}, f32[4,2,16]{2,1,0:T(2,128)S(1)}, u32[]{:S(2)}) copy-start(f32[4,2,16]{2,1,0:T(2,128)S(1)} %reduce_sum.38) | copy-start | bytes 1540
  47.3 3.6 %collective-permute-start.11 = (f32[4,16]{1,0:T(4,128)S(1)}, f32[4,16]{1,0:T(4,128)S(1)}, u32[]{:S(2)}, u32[]{:S(2)}) collective-permute-start(f32[4,16]{1,0:T(4,128)S(1)} %select_reduce_fusion), channel_id=1, source_target_pairs={{0,4},{4,0},{8,12},{12,8},{16,20},{20,16},{24,28},{28,24},{1,5},{5... | collective-permute-start | bytes 776 | tf_op jit(solution)/shard_map/ppermute | solution.py:108
  50.9 3.6 %collective-permute-start.12 = (f32[4,16]{1,0:T(4,128)S(1)}, f32[4,16]{1,0:T(4,128)S(1)}, u32[]{:S(2)}, u32[]{:S(2)}) collective-permute-start(f32[4,16]{1,0:T(4,128)S(1)} %add.623), channel_id=1, source_target_pairs={{0,8},{4,12},{8,0},{12,4},{16,24},{20,28},{24,16},{28,20},{1,9},{5... | collective-permute-start | bytes 776 | tf_op jit(solution)/shard_map/ppermute | solution.py:108
  54.5 4.5 %collective-permute-start.13 = (f32[4,16]{1,0:T(4,128)S(1)}, f32[4,16]{1,0:T(4,128)S(1)}, u32[]{:S(2)}, u32[]{:S(2)}) collective-permute-start(f32[4,16]{1,0:T(4,128)S(1)} %add.624), channel_id=1, source_target_pairs={{0,16},{4,20},{8,24},{12,28},{16,0},{20,4},{24,8},{28,12},{1,17},{... | collective-permute-start | bytes 776 | tf_op jit(solution)/shard_map/ppermute | solution.py:108
  59.0 1.2 %collective-permute-start.14 = (f32[4,16]{1,0:T(4,128)S(1)}, f32[4,16]{1,0:T(4,128)S(1)}, u32[]{:S(2)}, u32[]{:S(2)}) collective-permute-start(f32[4,16]{1,0:T(4,128)S(1)} %add.625), channel_id=1, source_target_pairs={{0,1},{1,0},{2,3},{3,2},{4,5},{5,4},{6,7},{7,6},{8,9},{9,8},{10,11... | collective-permute-start | bytes 776 | tf_op jit(solution)/shard_map/ppermute | solution.py:108
  60.2 5.4 %collective-permute-start.15 = (f32[4,16]{1,0:T(4,128)S(1)}, f32[4,16]{1,0:T(4,128)S(1)}, u32[]{:S(2)}, u32[]{:S(2)}) collective-permute-start(f32[4,16]{1,0:T(4,128)S(1)} %add.626), channel_id=1, source_target_pairs={{0,2},{1,3},{2,0},{3,1},{4,6},{5,7},{6,4},{7,5},{8,10},{9,11},{10,... | collective-permute-start | bytes 776 | tf_op jit(solution)/shard_map/ppermute | solution.py:108

commit v4 on v3

--- a/solution.py
+++ b/solution.py
@@ -126,7 +126,13 @@
 
     masked = solution * active[None]
     masked_grid = masked[:3].reshape(grid)
-    y_low, y_high = neighbour_shift(masked_grid, "gy", 2, 1)
+    weight_grid = (coupling * viscosity * active).reshape(1, row_count, y_cells, LAYERS)
+    basin_grid = jnp.broadcast_to(
+        basin_map.astype(jnp.float32)[None, :, :, None], (1, row_count, y_cells, LAYERS)
+    )
+    halo_source = jnp.concatenate([masked_grid, weight_grid, basin_grid], axis=0)
+    from_low, from_high = neighbour_shift(halo_source, "gy", 2, 1)
+    y_low, y_high = from_low[:3], from_high[:3]
     in_cell = in_cell_terms(masked, matrix)
     moving = in_cell[:3] + neighbour_terms(masked_grid, None, None, y_low, y_high, viscosity, frozen)
     residual = active[None] * (forcing - jnp.concatenate([moving, in_cell[3:]], axis=0))
@@ -161,17 +167,32 @@
     edge = (3, 1, y_cells, LAYERS)
     x_low2 = (near_masked[:, :1] + near_corr[:, :1]).reshape(edge)
     x_high2 = (near_masked[:, -1:] + near_corr[:, -1:]).reshape(edge)
-    y_low2, y_high2 = neighbour_shift(sm_grid, "gy", 2, 1)
+    no_cols = jnp.zeros((3, row_count, 1, LAYERS), jnp.float32)
     in_cell2 = in_cell_terms(smoothed_masked, matrix)
-    moving2 = in_cell2[:3] + neighbour_terms(sm_grid, x_low2, x_high2, y_low2, y_high2, viscosity, frozen)
+    moving2 = in_cell2[:3] + neighbour_terms(sm_grid, x_low2, x_high2, no_cols, no_cols, viscosity, frozen)
     post = active[None] * (forcing - jnp.concatenate([moving2, in_cell2[3:]], axis=0))
-
-    column_residual = jnp.sum(post.reshape(4, row_count, y_cells, LAYERS), axis=-1)
+    column_local = jnp.sum(post.reshape(4, row_count, y_cells, LAYERS), axis=-1)
+
+    to_low = jnp.sum(from_low[3:4, :, 0] * sm_grid[:, :, 0], axis=-1)
+    to_high = jnp.sum(from_high[3:4, :, 0] * sm_grid[:, :, -1], axis=-1)
+    count = lax.axis_size("gy")
+    forward = [(i, i + 1) for i in range(count - 1)]
+    backward = [(target, source) for source, target in forward]
+    for_last = lax.ppermute(to_low, "gy", backward)
+    for_first = lax.ppermute(to_high, "gy", forward)
+    edge_terms = jnp.zeros((3, row_count, y_cells), jnp.float32)
+    edge_terms = edge_terms.at[:, :, 0].set(for_first).at[:, :, -1].set(for_last)
+    column_residual = column_local + jnp.pad(edge_terms, ((0, 1), (0, 0), (0, 0)))
+
     basin_count = lax.axis_size("gx") // 2 * lax.axis_size("gy")
-    member = basin_map.reshape(-1)[:, None] == jnp.arange(basin_count, dtype=jnp.int32)[None, :]
-    partial_sums = jnp.sum(
-        jnp.where(member[None], column_residual.reshape(4, -1)[:, :, None], 0.0), axis=1
-    )
+    basin_ids = jnp.arange(basin_count, dtype=jnp.int32)
+    member = basin_map.reshape(-1)[:, None] == basin_ids[None, :]
+    partial_sums = jnp.sum(jnp.where(member[None], column_local.reshape(4, -1)[:, :, None], 0.0), axis=1)
+    beside_ids = jnp.concatenate([from_low[4, :, 0, 0], from_high[4, :, 0, 0]]).astype(jnp.int32)
+    beside_member = beside_ids[:, None] == basin_ids[None, :]
+    beside_terms = jnp.concatenate([to_low, to_high], axis=1)
+    beside_sums = jnp.sum(jnp.where(beside_member[None], beside_terms[:, :, None], 0.0), axis=1)
+    partial_sums = partial_sums + jnp.pad(beside_sums, ((0, 1), (0, 0)))
     basin_residual = tree_sum(tree_sum(partial_sums, "gx"), "gy")
     return (smoothed, column_residual, basin_residual)
 

time: 66.6 us -> 71.8 us (1.078)
  starting transfers between devices: 25.9 us -> 36.8 us
  waiting for transfers between devices: 26.7 us -> 18.5 us
  other arithmetic: 7.33 us -> 9.05 us
  local copies, waits for them, and re-layouts: 5.03 us -> 5.84 us
    ppermute x5, starting transfers between devices: 5.73 us -> 13.9 us  [tree_sum(): lax.ppermute(value, axis, [(i, i ^ step) for i in range(count)])]
    ppermute x5, waiting for transfers between devices: 12.5 us -> 4.55 us  [tree_sum(): lax.ppermute(value, axis, [(i, i ^ step) for i in range(count)])]
    ppermute x0 -> x2, starting transfers between devices: none -> 4.31 us  [the longest x1 3.03 us: local(): for_first = lax.ppermute(to_high, 'gy', forward)]
    ppermute x2 -> x1, starting transfers between devices: 5.66 us -> 2.4 us  [neighbour_shift(): lax.ppermute(lax.slice_in_dim(block, block.shape[dim] - width, None, axis...]
    ppermute x7, starting transfers between devices: 11.9 us -> 14.9 us  [gather_rows(): pieces.append(lax.ppermute(block, axis, pairs))]
    ppermute x2 -> x1, starting transfers between devices: 2.58 us -> 1.29 us  [neighbour_shift(): lax.ppermute(lax.slice_in_dim(block, 0, width, axis=dim), axis, backward)]
    convert_element_type x0 -> x2, other arithmetic: none -> 0.77 us  [the longest x1 0.69 us: local(): basin_map.astype(jnp.float32)[None, :, :, None]]
where the time goes in v4:
time: 71.8 us; the launch traced here: 71.4 us
  starting transfers between devices  36.8 us (51%)
  waiting for transfers between devices  18.5 us (26%)
  other arithmetic  9.05 us (13%)
  local copies, waits for them, and re-layouts  5.84 us (8%)
  between operations  1.22 us (2%)
    ppermute x7, starting transfers between devices, gather_rows(): pieces.append(lax.ppermute(block, axis, pairs))  14.9 us
    ppermute x5, starting transfers between devices, tree_sum(): lax.ppermute(value, axis, [(i, i ^ step) for i in range(count)])  13.9 us
    ppermute x7, waiting for transfers between devices, gather_rows(): pieces.append(lax.ppermute(block, axis, pairs))  13.5 us
    ppermute x5, waiting for transfers between devices, tree_sum(): lax.ppermute(value, axis, [(i, i ^ step) for i in range(count)])  4.55 us
    ppermute x1, starting transfers between devices, local(): for_first = lax.ppermute(to_high, 'gy', forward)  3.03 us
    ppermute x1, starting transfers between devices, neighbour_shift(): lax.ppermute(lax.slice_in_dim(block, block.shape[dim] - width, None, axis...  2.4 us
  transfers between devices with their start and end apart: 16, of which 8 were waited for; matrix products, arithmetic and copies ran while one was open for 7% of the time, Pallas kernels for 0%

profile of v4, /device:TPU:0, one launch (start us, length us, event | category | flops | bytes accessed | tf_op | source)
XLA Modules:
  0.0 71.4 jit_solution(7883316555886182222)
XLA Ops:
  0.6 0.7 convert_element_type.33
  1.4 0.7 %lt.38 = s32[2,16,80]{2,1,0:T(8,128)S(1)} broadcast(s32[2,16]{1,0:T(2,128)} %param.15), dimensions={0,1} | broadcast | bytes 10368 | tf_op jit(solution)/shard_map/lt | solution.py:119
  2.2 0.1 lt.39
  2.3 0.8 %broadcast_multiply_fusion.1 = f32[1,8,1280]{2,1,0:T(8,128)S(1)} fusion(f32[1,8,1280]{2,1,0:T(8,128)} %bitcast.112, f32[8,1280]{1,0:T(8,128)S(1)} %bitcast.111), kind=kLoop, calls=%fused_computation.60 | loop fusion | flops 10240 | bytes 122880 | tf_op jit(solution)/shard_map/mul | solution.py:127
  3.1 0.7 %select_bitcast_fusion = (f32[1,2,1280]{2,1,0:T(2,128)S(1)}, f32[2,1280]{1,0:T(2,128)S(1)}, f32[2,1280]{1,0:T(2,128)S(1)}, f32[2,1280]{1,0:T(2,128)S(1)}) fusion(pred[2,1280]{1,0:T(4,128)(4,1)S(1)} %get-tuple-element.98, f32[2,1280]{1,0:T(2,128)} %param.13), kind=kLoop, calls=%fused_computation.144 | loop fusion | flops 10240 | bytes 53760 | tf_op jit(solution)/shard_map/broadcast_in_dim | solution.py:142
  3.9 0.1 reshape.261
  4.1 2.4 %collective-permute-start = (f32[5,2,1,80]{3,2,1,0:T(1,128)S(1)}, f32[5,2,1,80]{3,2,1,0:T(1,128)S(1)}, u32[]{:S(2)}, u32[]{:S(2)}) collective-permute-start(f32[5,2,1,80]{3,2,1,0:T(1,128)S(1)} %get-tuple-element.105), channel_id=1, source_target_pairs={{0,1},{1,2},{2,3},{4,5},{5,6},{6,7},{8,9},{9,10},{10,11},{12,13},{... | collective-permute-start | bytes 9608 | tf_op jit(solution)/shard_map/ppermute | solution.py:16
  6.5 1.3 %collective-permute-start.1 = (f32[5,2,1,80]{3,2,1,0:T(1,128)S(1)}, f32[5,2,1,80]{3,2,1,0:T(1,128)S(1)}, u32[]{:S(2)}, u32[]{:S(2)}) collective-permute-start(f32[5,2,1,80]{3,2,1,0:T(1,128)S(1)} %get-tuple-element.106), channel_id=1, source_target_pairs={{1,0},{2,1},{3,2},{5,4},{6,5},{7,6},{9,8},{10,9},{11,10},{13,12},{... | collective-permute-start | bytes 9608 | tf_op jit(solution)/shard_map/ppermute | solution.py:17
  7.8 0.8 %eq.36 = s32[32]{0:T(128)S(1)} reshape(s32[2,16]{1,0:T(2,128)} %param.17) | data formatting | bytes 256 | tf_op jit(solution)/shard_map/eq | solution.py:189
  8.7 0.7 convert_subtract_fusion
  9.3 0.7 %slice_bitcast_fusion.6 = (f32[1,2,1280]{2,1,0:T(2,128)S(1)}, f32[1,2,1280]{2,1,0:T(2,128)S(1)}, f32[1,2,1280]{2,1,0:T(2,128)S(1)}) fusion(f32[4,4,2,1280]{3,2,1,0:T(2,128)} %bitcast.106), kind=kLoop, calls=%fused_computation.143 | loop fusion | bytes 61440 | tf_op jit(solution)/shard_map/stack;squeeze | solution.py:140
  10.2 1.0 %multiply_reduce_fusion.1 = f32[4,2,1280]{2,1,0:T(2,128)S(1)} fusion(f32[4,2,1280]{2,1,0:T(2,128)S(1)} %bitcast.109, f32[16,2,1280]{2,1,0:T(2,128)} %param.14), kind=kLoop, calls=%fused_computation.15 | loop fusion | flops 71680 | bytes 245760 | tf_op jit(solution)/shard_map/reduce_sum | solution.py:43
  11.2 0.5 collective-permute-done.1
  11.7 0.1 fusion.8
  11.8 0.1 reshape.263
  12.1 2.0 %collective-permute-start.7 = (f32[10,2,1280]{2,1,0:T(2,128)S(1)}, f32[10,2,1280]{2,1,0:T(2,128)S(1)}, u32[]{:S(2)}, u32[]{:S(2)}) collective-permute-start(f32[10,2,1280]{2,1,0:T(2,128)S(1)} %pad_maximum_fusion), channel_id=1, source_target_pairs={{24,0},{28,4},{0,8},{4,12},{8,16},{12,20},{16,24},{20,28},{25,1},{... | collective-permute-start | bytes 307208 | tf_op jit(solution)/shard_map/ppermute | solution.py:53
  14.1 2.5 %collective-permute-start.6 = (f32[10,2,1280]{2,1,0:T(2,128)S(1)}, f32[10,2,1280]{2,1,0:T(2,128)S(1)}, u32[]{:S(2)}, u32[]{:S(2)}) collective-permute-start(f32[10,2,1280]{2,1,0:T(2,128)S(1)} %pad_maximum_fusion), channel_id=1, source_target_pairs={{20,0},{24,4},{28,8},{0,12},{4,16},{8,20},{12,24},{16,28},{21,1},{... | collective-permute-start | bytes 307208 | tf_op jit(solution)/shard_map/ppermute | solution.py:53
  16.6 1.2 %collective-permute-start.5 = (f32[10,2,1280]{2,1,0:T(2,128)S(1)}, f32[10,2,1280]{2,1,0:T(2,128)S(1)}, u32[]{:S(2)}, u32[]{:S(2)}) collective-permute-start(f32[10,2,1280]{2,1,0:T(2,128)S(1)} %pad_maximum_fusion), channel_id=1, source_target_pairs={{16,0},{20,4},{24,8},{28,12},{0,16},{4,20},{8,24},{12,28},{17,1},{... | collective-permute-start | bytes 307208 | tf_op jit(solution)/shard_map/ppermute | solution.py:53
  17.8 2.7 %collective-permute-start.4 = (f32[10,2,1280]{2,1,0:T(2,128)S(1)}, f32[10,2,1280]{2,1,0:T(2,128)S(1)}, u32[]{:S(2)}, u32[]{:S(2)}) collective-permute-start(f32[10,2,1280]{2,1,0:T(2,128)S(1)} %pad_maximum_fusion), channel_id=1, source_target_pairs={{12,0},{16,4},{20,8},{24,12},{28,16},{0,20},{4,24},{8,28},{13,1},{... | collective-permute-start | bytes 307208 | tf_op jit(solution)/shard_map/ppermute | solution.py:53
  20.5 1.4 %collective-permute-start.2 = (f32[10,2,1280]{2,1,0:T(2,128)S(1)}, f32[10,2,1280]{2,1,0:T(2,128)S(1)}, u32[]{:S(2)}, u32[]{:S(2)}) collective-permute-start(f32[10,2,1280]{2,1,0:T(2,128)S(1)} %pad_maximum_fusion), channel_id=1, source_target_pairs={{4,0},{8,4},{12,8},{16,12},{20,16},{24,20},{28,24},{0,28},{5,1},{9... | collective-permute-start | bytes 307208 | tf_op jit(solution)/shard_map/ppermute | solution.py:53
  21.9 0.1 slice_reduce_fusion.17
  22.0 0.1 slice_reduce_fusion.16
  22.3 6.2 %collective-permute-done.2 = f32[10,2,1280]{2,1,0:T(2,128)S(1)} collective-permute-done((f32[10,2,1280]{2,1,0:T(2,128)S(1)}, f32[10,2,1280]{2,1,0:T(2,128)S(1)}, u32[]{:S(2)}, u32[]{:S(2)}) %collective-permute-start.2) | collective-permute-done | bytes 102432 | tf_op jit(solution)/shard_map/ppermute | solution.py:53
  28.5 5.2 %collective-permute-done.3 = f32[10,2,1280]{2,1,0:T(2,128)S(1)} collective-permute-done((f32[10,2,1280]{2,1,0:T(2,128)S(1)}, f32[10,2,1280]{2,1,0:T(2,128)S(1)}, u32[]{:S(2)}, u32[]{:S(2)}) %collective-permute-start.3) | collective-permute-done | bytes 102432 | tf_op jit(solution)/shard_map/ppermute | solution.py:53
  33.7 5.1 %collective-permute-start.8 = (f32[10,2,1280]{2,1,0:T(2,128)S(1)}, f32[10,2,1280]{2,1,0:T(2,128)S(1)}, u32[]{:S(2)}, u32[]{:S(2)}) collective-permute-start(f32[10,2,1280]{2,1,0:T(2,128)S(1)} %pad_maximum_fusion), channel_id=1, source_target_pairs={{28,0},{0,4},{4,8},{8,12},{12,16},{16,20},{20,24},{24,28},{29,1},{... | collective-permute-start | bytes 307208 | tf_op jit(solution)/shard_map/ppermute | solution.py:53
  38.9 2.1 %collective-permute-done.8 = f32[10,2,1280]{2,1,0:T(2,128)S(1)} collective-permute-done((f32[10,2,1280]{2,1,0:T(2,128)S(1)}, f32[10,2,1280]{2,1,0:T(2,128)S(1)}, u32[]{:S(2)}, u32[]{:S(2)}) %collective-permute-start.8) | collective-permute-done | bytes 102432 | tf_op jit(solution)/shard_map/ppermute | solution.py:53
  41.6 0.2 slice.427
  41.8 0.2 slice_reduce_fusion
  42.1 0.2 slice.421
  42.3 0.2 slice.418
  42.6 0.4 broadcast_divide_fusion
  43.0 0.6 fusion.15
  43.6 0.4 multiply_add_fusion
  44.0 0.4 stack.32
  44.5 0.7 broadcast_multiply_fusion
  45.2 0.1 reshape.264
  45.5 0.2 fusion.30
  45.7 0.1 reshape.265
  45.8 0.1 reshape.266
  45.9 0.1 fusion.5
  46.0 0.1 reshape.267
  46.1 0.1 reshape.268
  46.3 0.1 reshape.269
  46.4 0.1 reduce_sum.65
  46.5 0.1 broadcast_in_dim.94
  46.6 0.1 multiply_reduce_fusion.3
  46.7 0.1 select_reduce_fusion.1
  46.8 0.1 select_reduce_fusion
  46.9 2.4 %collective-permute-start.11 = (f32[4,16]{1,0:T(4,128)S(1)}, f32[4,16]{1,0:T(4,128)S(1)}, u32[]{:S(2)}, u32[]{:S(2)}) collective-permute-start(f32[4,16]{1,0:T(4,128)S(1)} %pad_add_fusion.1), channel_id=1, source_target_pairs={{0,4},{4,0},{8,12},{12,8},{16,20},{20,16},{24,28},{28,24},{1,5},{5... | collective-permute-start | bytes 776 | tf_op jit(solution)/shard_map/ppermute | solution.py:108
  49.4 1.6 %collective-permute-done.11 = f32[4,16]{1,0:T(4,128)S(1)} collective-permute-done((f32[4,16]{1,0:T(4,128)S(1)}, f32[4,16]{1,0:T(4,128)S(1)}, u32[]{:S(2)}, u32[]{:S(2)}) %collective-permute-start.11) | collective-permute-done | bytes 288 | tf_op jit(solution)/shard_map/ppermute | solution.py:108
  50.9 4.0 %collective-permute-start.12 = (f32[4,16]{1,0:T(4,128)S(1)}, f32[4,16]{1,0:T(4,128)S(1)}, u32[]{:S(2)}, u32[]{:S(2)}) collective-permute-start(f32[4,16]{1,0:T(4,128)S(1)} %add.645), channel_id=1, source_target_pairs={{0,8},{4,12},{8,0},{12,4},{16,24},{20,28},{24,16},{28,20},{1,9},{5... | collective-permute-start | bytes 776 | tf_op jit(solution)/shard_map/ppermute | solution.py:108
  54.9 1.6 %collective-permute-done.12 = f32[4,16]{1,0:T(4,128)S(1)} collective-permute-done((f32[4,16]{1,0:T(4,128)S(1)}, f32[4,16]{1,0:T(4,128)S(1)}, u32[]{:S(2)}, u32[]{:S(2)}) %collective-permute-start.12) | collective-permute-done | bytes 288 | tf_op jit(solution)/shard_map/ppermute | solution.py:108
  56.5 2.9 %collective-permute-start.13 = (f32[4,16]{1,0:T(4,128)S(1)}, f32[4,16]{1,0:T(4,128)S(1)}, u32[]{:S(2)}, u32[]{:S(2)}) collective-permute-start(f32[4,16]{1,0:T(4,128)S(1)} %add.646), channel_id=1, source_target_pairs={{0,16},{4,20},{8,24},{12,28},{16,0},{20,4},{24,8},{28,12},{1,17},{... | collective-permute-start | bytes 776 | tf_op jit(solution)/shard_map/ppermute | solution.py:108
  59.4 1.3 %collective-permute-start.10 = (f32[3,2]{1,0:T(4,128)S(1)}, f32[3,2]{1,0:T(4,128)S(1)}, u32[]{:S(2)}, u32[]{:S(2)}) collective-permute-start(f32[3,2]{1,0:T(4,128)S(1)} %get-tuple-element.121), channel_id=1, source_target_pairs={{1,0},{2,1},{3,2},{5,4},{6,5},{7,6},{9,8},{10,9},{11,10},{13,12},{... | collective-permute-start | bytes 80 | tf_op jit(solution)/shard_map/ppermute | solution.py:181
  60.7 3.0 %collective-permute-start.9 = (f32[3,2]{1,0:T(4,128)S(1)}, f32[3,2]{1,0:T(4,128)S(1)}, u32[]{:S(2)}, u32[]{:S(2)}) collective-permute-start(f32[3,2]{1,0:T(4,128)S(1)} %get-tuple-element.122), channel_id=1, source_target_pairs={{0,1},{1,2},{2,3},{4,5},{5,6},{6,7},{8,9},{9,10},{10,11},{12,13},{... | collective-permute-start | bytes 80 | tf_op jit(solution)/shard_map/ppermute | solution.py:182
  63.7 0.1 copy.45
  63.8 2.2 %collective-permute-start.14 = (f32[4,16]{1,0:T(4,128)S(1)}, f32[4,16]{1,0:T(4,128)S(1)}, u32[]{:S(2)}, u32[]{:S(2)}) collective-permute-start(f32[4,16]{1,0:T(4,128)S(1)} %add.647), channel_id=1, source_target_pairs={{0,1},{1,0},{2,3},{3,2},{4,5},{5,4},{6,7},{7,6},{8,9},{9,8},{10,11... | collective-permute-start | bytes 776 | tf_op jit(solution)/shard_map/ppermute | solution.py:108
  66.1 0.1 copy.43
  66.2 0.2 scatter.9
  66.4 0.5 collective-permute-done.14
  66.9 2.3 %collective-permute-start.15 = (f32[4,16]{1,0:T(4,128)S(1)}, f32[4,16]{1,0:T(4,128)S(1)}, u32[]{:S(2)}, u32[]{:S(2)}) collective-permute-start(f32[4,16]{1,0:T(4,128)S(1)} %add.648), channel_id=1, source_target_pairs={{0,2},{1,3},{2,0},{3,1},{4,6},{5,7},{6,4},{7,5},{8,10},{9,11},{10,... | collective-permute-start | bytes 776 | tf_op jit(solution)/shard_map/ppermute | solution.py:108
  69.2 0.6 pad_add_fusion
  69.8 1.0 %collective-permute-done.15 = f32[4,16]{1,0:T(4,128)S(1)} collective-permute-done((f32[4,16]{1,0:T(4,128)S(1)}, f32[4,16]{1,0:T(4,128)S(1)}, u32[]{:S(2)}, u32[]{:S(2)}) %collective-permute-start.15) | collective-permute-done | bytes 288 | tf_op jit(solution)/shard_map/ppermute | solution.py:108
  70.8 0.6 add.649
  (87 shorter events, 2.0 us)
Async XLA Ops:
  0.6 11.3 %copy-start.1 = (f32[4,2,1280]{2,1,0:T(2,128)S(1)}, f32[4,2,1280]{2,1,0:T(2,128)}, u32[]{:S(2)}) copy-start(f32[4,2,1280]{2,1,0:T(2,128)} %param.12) | copy-start | bytes 122884
  4.1 7.1 %collective-permute-start = (f32[5,2,1,80]{3,2,1,0:T(1,128)S(1)}, f32[5,2,1,80]{3,2,1,0:T(1,128)S(1)}, u32[]{:S(2)}, u32[]{:S(2)}) collective-permute-start(f32[5,2,1,80]{3,2,1,0:T(1,128)S(1)} %get-tuple-element.105), channel_id=1, source_target_pairs={{0,1},{1,2},{2,3},{4,5},{5,6},{6,7},{8,9},{9,10},{10,11},{12,13},{... | collective-permute-start | bytes 9608 | tf_op jit(solution)/shard_map/ppermute | solution.py:16
  6.5 5.2 %collective-permute-start.1 = (f32[5,2,1,80]{3,2,1,0:T(1,128)S(1)}, f32[5,2,1,80]{3,2,1,0:T(1,128)S(1)}, u32[]{:S(2)}, u32[]{:S(2)}) collective-permute-start(f32[5,2,1,80]{3,2,1,0:T(1,128)S(1)} %get-tuple-element.106), channel_id=1, source_target_pairs={{1,0},{2,1},{3,2},{5,4},{6,5},{7,6},{9,8},{10,9},{11,10},{13,12},{... | collective-permute-start | bytes 9608 | tf_op jit(solution)/shard_map/ppermute | solution.py:17
  11.2 30.0 %copy-start.4 = (f32[5,2,1,80]{3,2,1,0:T(1,128)}, f32[5,2,1,80]{3,2,1,0:T(1,128)S(1)}, u32[]{:S(2)}) copy-start(f32[5,2,1,80]{3,2,1,0:T(1,128)S(1)} %collective-permute-done) | copy-start | bytes 9604
  11.7 29.5 %copy-start.5 = (f32[5,2,1,80]{3,2,1,0:T(1,128)}, f32[5,2,1,80]{3,2,1,0:T(1,128)S(1)}, u32[]{:S(2)}) copy-start(f32[5,2,1,80]{3,2,1,0:T(1,128)S(1)} %collective-permute-done.1) | copy-start | bytes 9604
  12.1 26.8 %collective-permute-start.7 = (f32[10,2,1280]{2,1,0:T(2,128)S(1)}, f32[10,2,1280]{2,1,0:T(2,128)S(1)}, u32[]{:S(2)}, u32[]{:S(2)}) collective-permute-start(f32[10,2,1280]{2,1,0:T(2,128)S(1)} %pad_maximum_fusion), channel_id=1, source_target_pairs={{24,0},{28,4},{0,8},{4,12},{8,16},{12,20},{16,24},{20,28},{25,1},{... | collective-permute-start | bytes 307208 | tf_op jit(solution)/shard_map/ppermute | solution.py:53
  14.1 24.8 %collective-permute-start.6 = (f32[10,2,1280]{2,1,0:T(2,128)S(1)}, f32[10,2,1280]{2,1,0:T(2,128)S(1)}, u32[]{:S(2)}, u32[]{:S(2)}) collective-permute-start(f32[10,2,1280]{2,1,0:T(2,128)S(1)} %pad_maximum_fusion), channel_id=1, source_target_pairs={{20,0},{24,4},{28,8},{0,12},{4,16},{8,20},{12,24},{16,28},{21,1},{... | collective-permute-start | bytes 307208 | tf_op jit(solution)/shard_map/ppermute | solution.py:53
  16.6 22.2 %collective-permute-start.5 = (f32[10,2,1280]{2,1,0:T(2,128)S(1)}, f32[10,2,1280]{2,1,0:T(2,128)S(1)}, u32[]{:S(2)}, u32[]{:S(2)}) collective-permute-start(f32[10,2,1280]{2,1,0:T(2,128)S(1)} %pad_maximum_fusion), channel_id=1, source_target_pairs={{16,0},{20,4},{24,8},{28,12},{0,16},{4,20},{8,24},{12,28},{17,1},{... | collective-permute-start | bytes 307208 | tf_op jit(solution)/shard_map/ppermute | solution.py:53
  17.8 21.0 %collective-permute-start.4 = (f32[10,2,1280]{2,1,0:T(2,128)S(1)}, f32[10,2,1280]{2,1,0:T(2,128)S(1)}, u32[]{:S(2)}, u32[]{:S(2)}) collective-permute-start(f32[10,2,1280]{2,1,0:T(2,128)S(1)} %pad_maximum_fusion), channel_id=1, source_target_pairs={{12,0},{16,4},{20,8},{24,12},{28,16},{0,20},{4,24},{8,28},{13,1},{... | collective-permute-start | bytes 307208 | tf_op jit(solution)/shard_map/ppermute | solution.py:53
  20.5 8.0 %collective-permute-start.2 = (f32[10,2,1280]{2,1,0:T(2,128)S(1)}, f32[10,2,1280]{2,1,0:T(2,128)S(1)}, u32[]{:S(2)}, u32[]{:S(2)}) collective-permute-start(f32[10,2,1280]{2,1,0:T(2,128)S(1)} %pad_maximum_fusion), channel_id=1, source_target_pairs={{4,0},{8,4},{12,8},{16,12},{20,16},{24,20},{28,24},{0,28},{5,1},{9... | collective-permute-start | bytes 307208 | tf_op jit(solution)/shard_map/ppermute | solution.py:53
  28.5 5.2 %collective-permute-start.3 = (f32[10,2,1280]{2,1,0:T(2,128)S(1)}, f32[10,2,1280]{2,1,0:T(2,128)S(1)}, u32[]{:S(2)}, u32[]{:S(2)}) collective-permute-start(f32[10,2,1280]{2,1,0:T(2,128)S(1)} %pad_maximum_fusion), channel_id=1, source_target_pairs={{8,0},{12,4},{16,8},{20,12},{24,16},{28,20},{0,24},{4,28},{9,1},{1... | collective-permute-start | bytes 307208 | tf_op jit(solution)/shard_map/ppermute | solution.py:53
  33.7 7.4 %collective-permute-start.8 = (f32[10,2,1280]{2,1,0:T(2,128)S(1)}, f32[10,2,1280]{2,1,0:T(2,128)S(1)}, u32[]{:S(2)}, u32[]{:S(2)}) collective-permute-start(f32[10,2,1280]{2,1,0:T(2,128)S(1)} %pad_maximum_fusion), channel_id=1, source_target_pairs={{28,0},{0,4},{4,8},{8,12},{12,16},{16,20},{20,24},{24,28},{29,1},{... | collective-permute-start | bytes 307208 | tf_op jit(solution)/shard_map/ppermute | solution.py:53
  42.5 1.9 %copy-start = (f32[16,2,1280]{2,1,0:T(2,128)S(1)}, f32[16,2,1280]{2,1,0:T(2,128)}, u32[]{:S(2)}) copy-start(f32[16,2,1280]{2,1,0:T(2,128)} %param.14) | copy-start | bytes 491524
  42.5 1.9 %copy-start.3 = (f32[2,1280]{1,0:T(2,128)S(1)}, f32[2,1280]{1,0:T(2,128)}, u32[]{:S(2)}) copy-start(f32[2,1280]{1,0:T(2,128)} %param.13) | copy-start | bytes 30724
  42.5 2.0 %copy-start.2 = (f32[4,2,1280]{2,1,0:T(2,128)S(1)}, f32[4,2,1280]{2,1,0:T(2,128)}, u32[]{:S(2)}) copy-start(f32[4,2,1280]{2,1,0:T(2,128)} %param.11) | copy-start | bytes 122884
  44.4 2.2 %slice-start = ((f32[5,2,1,80]{3,2,1,0:T(1,128)}), f32[1,2,1,80]{3,2,1,0:T(1,128)S(1)}, s32[]{:S(2)}) async-start(f32[5,2,1,80]{3,2,1,0:T(1,128)} %copy-done.4), calls=%async_computation | async-start | bytes 2048 | tf_op jit(solution)/shard_map/slice | solution.py:176
  44.4 2.2 %slice-start.1 = ((f32[5,2,1,80]{3,2,1,0:T(1,128)}), f32[1,2,1,80]{3,2,1,0:T(1,128)S(1)}, s32[]{:S(2)}) async-start(f32[5,2,1,80]{3,2,1,0:T(1,128)} %copy-done.5), calls=%async_computation.1 | async-start | bytes 2048 | tf_op jit(solution)/shard_map/slice | solution.py:177
  46.9 4.0 %collective-permute-start.11 = (f32[4,16]{1,0:T(4,128)S(1)}, f32[4,16]{1,0:T(4,128)S(1)}, u32[]{:S(2)}, u32[]{:S(2)}) collective-permute-start(f32[4,16]{1,0:T(4,128)S(1)} %pad_add_fusion.1), channel_id=1, source_target_pairs={{0,4},{4,0},{8,12},{12,8},{16,20},{20,16},{24,28},{28,24},{1,5},{5... | collective-permute-start | bytes 776 | tf_op jit(solution)/shard_map/ppermute | solution.py:108
  50.9 5.5 %collective-permute-start.12 = (f32[4,16]{1,0:T(4,128)S(1)}, f32[4,16]{1,0:T(4,128)S(1)}, u32[]{:S(2)}, u32[]{:S(2)}) collective-permute-start(f32[4,16]{1,0:T(4,128)S(1)} %add.645), channel_id=1, source_target_pairs={{0,8},{4,12},{8,0},{12,4},{16,24},{20,28},{24,16},{28,20},{1,9},{5... | collective-permute-start | bytes 776 | tf_op jit(solution)/shard_map/ppermute | solution.py:108
  56.5 7.4 %collective-permute-start.13 = (f32[4,16]{1,0:T(4,128)S(1)}, f32[4,16]{1,0:T(4,128)S(1)}, u32[]{:S(2)}, u32[]{:S(2)}) collective-permute-start(f32[4,16]{1,0:T(4,128)S(1)} %add.646), channel_id=1, source_target_pairs={{0,16},{4,20},{8,24},{12,28},{16,0},{20,4},{24,8},{28,12},{1,17},{... | collective-permute-start | bytes 776 | tf_op jit(solution)/shard_map/ppermute | solution.py:108
  59.4 4.3 %collective-permute-start.10 = (f32[3,2]{1,0:T(4,128)S(1)}, f32[3,2]{1,0:T(4,128)S(1)}, u32[]{:S(2)}, u32[]{:S(2)}) collective-permute-start(f32[3,2]{1,0:T(4,128)S(1)} %get-tuple-element.121), channel_id=1, source_target_pairs={{1,0},{2,1},{3,2},{5,4},{6,5},{7,6},{9,8},{10,9},{11,10},{13,12},{... | collective-permute-start | bytes 80 | tf_op jit(solution)/shard_map/ppermute | solution.py:181
  60.7 5.4 %collective-permute-start.9 = (f32[3,2]{1,0:T(4,128)S(1)}, f32[3,2]{1,0:T(4,128)S(1)}, u32[]{:S(2)}, u32[]{:S(2)}) collective-permute-start(f32[3,2]{1,0:T(4,128)S(1)} %get-tuple-element.122), channel_id=1, source_target_pairs={{0,1},{1,2},{2,3},{4,5},{5,6},{6,7},{8,9},{9,10},{10,11},{12,13},{... | collective-permute-start | bytes 80 | tf_op jit(solution)/shard_map/ppermute | solution.py:182
  63.8 3.1 %collective-permute-start.14 = (f32[4,16]{1,0:T(4,128)S(1)}, f32[4,16]{1,0:T(4,128)S(1)}, u32[]{:S(2)}, u32[]{:S(2)}) collective-permute-start(f32[4,16]{1,0:T(4,128)S(1)} %add.647), channel_id=1, source_target_pairs={{0,1},{1,0},{2,3},{3,2},{4,5},{5,4},{6,7},{7,6},{8,9},{9,8},{10,11... | collective-permute-start | bytes 776 | tf_op jit(solution)/shard_map/ppermute | solution.py:108
  66.9 3.9 %collective-permute-start.15 = (f32[4,16]{1,0:T(4,128)S(1)}, f32[4,16]{1,0:T(4,128)S(1)}, u32[]{:S(2)}, u32[]{:S(2)}) collective-permute-start(f32[4,16]{1,0:T(4,128)S(1)} %add.648), channel_id=1, source_target_pairs={{0,2},{1,3},{2,0},{3,1},{4,6},{5,7},{6,4},{7,5},{8,10},{9,11},{10,... | collective-permute-start | bytes 776 | tf_op jit(solution)/shard_map/ppermute | solution.py:108
